TPU v7x, 128 devices: a whole 4x4x4 slice. The times are simulated.
128 devices in a mesh: rep: 4 (over x), fsdp: 2 (over core), tp: 16 (over z, y).
Axes of the slice: x: 4, y: 4, z: 4, core: 2. Of those that a mesh axis runs over, the one named last changes fastest.
Arguments:
- tokens: bfloat16 [8192, 2048], P(('rep', 'fsdp'), 'tp'), may hold values from -6 to 6
- cotangent: bfloat16 [8192, 2048], P(('rep', 'fsdp'), 'tp'), may hold values from -6 to 6
- frame_mask: int32 [8192], P(('rep', 'fsdp')), may hold values 0 or 1
- ln_gain: bfloat16 [2048], P('tp'), may hold values from 0.099609375 to 1.8984375
- ln_bias: bfloat16 [2048], P('tp'), may hold values from -3 to 3
- weight_in: bfloat16 [2048, 8192], P('fsdp', 'tp'), may hold values from -0.1875 to 0.1875
- weight_out: bfloat16 [8192, 2048], P('tp', 'fsdp'), may hold values from -0.09375 to 0.09375
- blocks_in: int32 [16, 64], P('fsdp', 'tp'), may hold values 0 or 1
- blocks_out: int32 [64, 16], P('tp', 'fsdp'), may hold values 0 or 1
Outputs:
- block_out: bfloat16 [8192, 2048], P(('rep', 'fsdp'), 'tp')
- input_grad: bfloat16 [8192, 2048], P(('rep', 'fsdp'), 'tp')
- grad_in: float32 [2048, 8192], P('fsdp', 'tp')
- grad_out: float32 [8192, 2048], P('tp', 'fsdp')
- grad_gain: float32 [2048], P('tp')
- grad_bias: float32 [2048], P('tp')
All inputs are finite; a program needn't handle non-finite values. No bound on the sum of `frame_mask` or of `blocks_in` or of `blocks_out` on one device may be relied on, other than what follows from the above.
Results may differ from a plain program's by a relative error of at most 0.019.
Values may be sent and summed in bfloat16 or wider, within the bound.
No kernel may reach another device: no remote copies, remote signals or barrier semaphores. Data moves between devices by JAX's collectives and lax.ppermute only.
A program may use at most 128 MiB of HBM per device.

v0:
```python
from functools import partial

import jax
import jax.numpy as jnp
from jax import lax
from jax.sharding import PartitionSpec as P

BLK = 128


def apply_blocks(weight, blocks, kind):
    row_blocks, col_blocks = blocks.shape
    shaped = weight.reshape(row_blocks, BLK, col_blocks, BLK)
    keeper = blocks.astype(kind)[:, None, :, None]
    return (shaped * keeper).reshape(weight.shape)


def contract_rows(left, right):
    return lax.dot_general(
        left, right, (((0,), (0,)), ((), ())), preferred_element_type=jnp.float32
    )


def contract_cols(left, right):
    return lax.dot_general(
        left, right, (((1,), (1,)), ((), ())), preferred_element_type=jnp.float32
    )


def pair_gather(own, axis):
    other = lax.ppermute(own, "fsdp", perm=[(0, 1), (1, 0)])
    first = lax.axis_index("fsdp") == 0
    low = jnp.where(first, own, other)
    high = jnp.where(first, other, own)
    return jnp.concatenate([low, high], axis=axis)


def pair_scatter(term, axis):
    half = term.shape[axis] // 2
    idx = lax.axis_index("fsdp")
    keep = lax.dynamic_slice_in_dim(term, idx * half, half, axis)
    send = lax.dynamic_slice_in_dim(term, (1 - idx) * half, half, axis)
    recv = lax.ppermute(send, "fsdp", perm=[(0, 1), (1, 0)])
    return keep.astype(jnp.float32) + recv.astype(jnp.float32)


def rows_allreduce(term, axis, size):
    rows = term.shape[0] // size
    mine = lax.all_to_all(term.astype(jnp.bfloat16), axis, split_axis=0, concat_axis=0, tiled=True)
    reduced = jnp.sum(mine.reshape(size, rows, -1).astype(jnp.float32), axis=0)
    reduced = reduced.astype(jnp.bfloat16)
    copies = jnp.broadcast_to(reduced[None], (size,) + reduced.shape).reshape(term.shape)
    whole = lax.all_to_all(copies, axis, split_axis=0, concat_axis=0, tiled=True)
    return whole.astype(jnp.float32)


def butterfly_sum(values, axis, size):
    bit = 1
    while bit < size:
        perm = [(i, i ^ bit) for i in range(size)]
        values = values + lax.ppermute(values, axis, perm=perm)
        bit *= 2
    return values


def on_device(
    sizes,
    tokens, cotangent, frame_mask, ln_gain, ln_bias, weight_in, weight_out, blocks_in, blocks_out
):
    frames = tokens.shape[0]
    stacked = jnp.concatenate(
        [tokens, ln_gain[None], ln_bias[None], jnp.zeros((6, tokens.shape[1]), tokens.dtype)]
    )
    gathered = lax.all_to_all(
        jnp.tile(stacked, (1, sizes["tp"])), "tp", split_axis=1, concat_axis=1, tiled=True
    )
    whole_rows = gathered[:frames]
    gain_full, bias_full = gathered[frames], gathered[frames + 1]
    masked_in = apply_blocks(weight_in, blocks_in, jnp.bfloat16)
    masked_out = apply_blocks(weight_out, blocks_out, jnp.bfloat16)
    full_in = pair_gather(masked_in, 0)
    full_out = pair_gather(masked_out, 1)
    width = whole_rows.shape[1]
    own_width = tokens.shape[1]
    col_start = lax.axis_index("tp") * own_width
    gelu_exact = partial(jax.nn.gelu, approximate=False)
    values = whole_rows.astype(jnp.float32)
    centre = jnp.mean(values, axis=1, keepdims=True)
    centred = values - centre
    inv_std = lax.rsqrt(jnp.mean(centred * centred, axis=1, keepdims=True) + 1e-05)
    normed = centred * inv_std
    gain_f = gain_full.astype(jnp.float32)
    scaled = (normed * gain_f + bias_full.astype(jnp.float32)).astype(jnp.bfloat16)
    hidden = jnp.dot(scaled, full_in, preferred_element_type=jnp.float32)
    active = gelu_exact(hidden).astype(jnp.bfloat16)
    partial_out = lax.dot_general(
        full_out, active, (((0,), (1,)), ((), ())), preferred_element_type=jnp.float32
    ).astype(jnp.bfloat16)
    whole_grad = lax.all_gather(cotangent, "tp", axis=1, tiled=True)
    unused, whole_grad = lax.optimization_barrier((partial_out, whole_grad))
    branch = lax.psum_scatter(
        partial_out, "tp", scatter_dimension=0, tiled=True
    ).astype(jnp.float32).T
    flags = frame_mask[:, None].astype(jnp.bfloat16)
    chosen = whole_grad * flags
    chosen_own = cotangent * flags
    back_active = contract_cols(chosen, full_out)
    unused, gelu_back = jax.vjp(gelu_exact, hidden)
    back_hidden = gelu_back(back_active)[0].astype(jnp.bfloat16)
    partial_normed = contract_cols(back_hidden, full_in).astype(jnp.bfloat16)
    back_normed = lax.psum_scatter(
        partial_normed, "tp", scatter_dimension=1, tiled=True
    ).astype(jnp.float32)
    piece = partial_normed.astype(jnp.float32)
    piece_scaled = piece * gain_f
    row_sums = jnp.stack([jnp.sum(piece_scaled, axis=1), jnp.sum(piece_scaled * normed, axis=1)])
    col_sums = jnp.stack([jnp.sum(piece * normed, axis=0), jnp.sum(piece, axis=0)])
    both_sums = butterfly_sum(jnp.concatenate([row_sums, col_sums], axis=1), "tp", sizes["tp"])
    row_sums, col_sums = both_sums[:, :frames], both_sums[:, frames:]
    sum_plain, sum_cross = row_sums[0], row_sums[1]
    for name in ("fsdp", "rep"):
        col_sums = butterfly_sum(col_sums, name, sizes[name])
    whole_gain, whole_bias = col_sums[0], col_sums[1]
    grad_gain = lax.dynamic_slice_in_dim(whole_gain, col_start, own_width, 0)
    grad_bias = lax.dynamic_slice_in_dim(whole_bias, col_start, own_width, 0)
    term_in = contract_rows(scaled, back_hidden).astype(jnp.bfloat16)
    term_out = contract_rows(active, chosen).astype(jnp.bfloat16)
    shard_in = pair_scatter(term_in, 0)
    shard_out = pair_scatter(term_out, 1)
    shard_in, shard_out, branch = lax.optimization_barrier((shard_in, shard_out, branch))
    block_out = (tokens.astype(jnp.float32) + branch).astype(jnp.bfloat16)
    shard_in = rows_allreduce(shard_in, "rep", sizes["rep"])
    shard_out = rows_allreduce(shard_out, "rep", sizes["rep"])
    grad_in = apply_blocks(shard_in, blocks_in, jnp.float32)
    grad_out = apply_blocks(shard_out, blocks_out, jnp.float32)
    grad_in, grad_out, back_normed = lax.optimization_barrier((grad_in, grad_out, back_normed))
    normed_own = lax.dynamic_slice_in_dim(normed, col_start, own_width, 1)
    gain_own = ln_gain.astype(jnp.float32)
    back_scaled = back_normed * gain_own
    mean_plain = (sum_plain / width)[:, None]
    mean_cross = (sum_cross / width)[:, None]
    back_rows = inv_std * (back_scaled - mean_plain - normed_own * mean_cross)
    input_grad = (chosen_own.astype(jnp.float32) + back_rows).astype(jnp.bfloat16)
    return (block_out, input_grad, grad_in, grad_out, grad_gain, grad_bias)


def solution(mesh):
    placed = (
        P(("rep", "fsdp"), "tp"),
        P(("rep", "fsdp"), "tp"),
        P(("rep", "fsdp")),
        P("tp"),
        P("tp"),
        P("fsdp", "tp"),
        P("tp", "fsdp"),
        P("fsdp", "tp"),
        P("tp", "fsdp"),
    )
    return jax.shard_map(
        partial(on_device, dict(mesh.shape)),
        mesh=mesh,
        in_specs=placed,
        out_specs=(
            P(("rep", "fsdp"), "tp"),
            P(("rep", "fsdp"), "tp"),
            P("fsdp", "tp"),
            P("tp", "fsdp"),
            P("tp"),
            P("tp"),
        ),
        check_vma=False,
    )
```

profile of v0, /device:TPU:0, one launch (start us, length us, event | category | flops | bytes accessed | tf_op | source)
XLA Modules:
  0.0 284.5 jit_solution(11658933866755518234)
XLA Ops:
  7.2 1.7 concatenate.12
  8.9 2.5 tile.2
  11.4 8.3 %all-to-all-start = ((bf16[1032,16,128]{2,0,1:T(8,128)(2,1)}), bf16[1032,16,128]{2,0,1:T(8,128)(2,1)}, u32[]{:S(2)}, u32[]{:S(2)}) async-start(bf16[1032,16,128]{2,0,1:T(8,128)(2,1)} %tile.2), calls=%async_computation | async-start | bytes 8454144 | tf_op jit(solution)/shard_map/all_to_all | solution.py:74
  19.8 0.7 all-gather.2.cloned.1.call-update
  20.6 0.3 mul.164
  21.3 0.2 mul.168
  21.5 0.7 copy-done.3
  22.4 1.6 collective-permute-done
  24.0 2.3 broadcast_select_fusion.3
  26.4 2.7 broadcast_select_fusion.1
  29.1 57.2 %all-to-all-done = bf16[1032,16,128]{2,0,1:T(8,128)(2,1)} async-done(((bf16[1032,16,128]{2,0,1:T(8,128)(2,1)}), bf16[1032,16,128]{2,0,1:T(8,128)(2,1)}, u32[]{:S(2)}, u32[]{:S(2)}) %all-to-all-start) | async-done | bytes 4227104 | tf_op jit(solution)/shard_map/all_to_all | solution.py:74
  86.2 3.0 %convert_reduce_fusion = f32[1024]{0:T(1024)S(1)} fusion(bf16[1032,16,128]{2,0,1:T(8,128)(2,1)} %all-to-all-done), kind=kLoop, calls=%fused_computation.1 | loop fusion | flops 4193280 | bytes 4198400 | tf_op jit(solution)/shard_map/reduce_sum | solution.py:88
  89.2 3.2 %fusion.5 = f32[1024]{0:T(1024)S(1)} fusion(f32[1024]{0:T(1024)S(1)} %broadcast_multiply_fusion, bf16[1032,16,128]{2,0,1:T(8,128)(2,1)} %all-to-all-done), kind=kLoop, calls=%fused_computation.11 | loop fusion | flops 8387584 | bytes 4202496 | tf_op jit(solution)/shard_map/reduce_sum | solution.py:90
  92.4 0.8 slice_convert_fusion.1
  93.3 10.0 %multiply_convert_fusion = (bf16[1024,512]{1,0:T(8,128)(2,1)S(1)}, f32[1024,512]{1,0:T(8,128)}, f32[1024,512]{1,0:T(8,128)}) fusion(bf16[1024,512]{1,0:T(8,128)(2,1)S(1)} %copy-done.4, bf16[1024,512]{1,0:T(8,128)(2,1)S(1)} %get-tuple-element.42, f32[2048]{0:T(1024)S(1)} %bitcast.92, f32[2048]{0:T(1024)S(1)} %bitcast.89, f32[1024]{0:T(1024)S(1)} %add_rsqrt_fusion, ...), kind=kOutput, calls=%fused_computation.34 | convolution fusion | flops 2198339584 | bytes 11558912 | tf_op jit(solution)/shard_map/dot_general | solution.py:94
  103.3 1.0 copy-done.13
  104.3 4.4 %convolution_convert_fusion.1 = bf16[2048,1024]{1,0:T(8,128)(2,1)} fusion(bf16[1024,512]{1,0:T(8,128)(2,1)S(1)} %get-tuple-element.36, bf16[512,1024]{1,0:T(8,128)(2,1)S(1)} %copy-done.6, bf16[512,1024]{1,0:T(8,128)(2,1)S(1)} %copy-done.5), kind=kOutput, calls=%fused_computation.16 | convolution fusion | flops 2153775104 | bytes 7340032 | tf_op jit(solution)/shard_map/dot_general | solution.py:96
  108.7 0.2 reduce-scatter.7.cloned.1.call-start
  108.9 0.4 copy-done.9
  109.4 3.7 %all-gather.2.cloned.1.call-done = bf16[1024,2048]{1,0:T(8,128)(2,1)} async-done(((bf16[1024,128]{1,0:T(8,128)(2,1)}), bf16[1024,2048]{1,0:T(8,128)(2,1)}) %all-gather.2.cloned.1.call-update) | async-done | bytes 4194320 | tf_op jit(solution)/shard_map/all_gather | solution.py:99
  113.1 6.7 %add_convert_fusion.1 = bf16[1024,512]{1,0:T(8,128)(2,1)S(1)} fusion(f32[1024,512]{1,0:T(8,128)} %get-tuple-element.37, f32[1024,512]{1,0:T(8,128)} %get-tuple-element.52, bf16[1024,2048]{1,0:T(8,128)(2,1)} %all-gather.2.cloned.1.call-done, bf16[1024]{0:T(1024)(128)(2,1)S(1)} %convert_element_type.140, bf16[512,1024]{1,0:T(8,128)(2,1)} %get-tuple-element.41, ...), kind=kOutput, calls=%fused_computation.31 | convolution fusion | flops 2161115136 | bytes 11536384 | tf_op jit(solution)/shard_map/dot_general | solution.py:25
  119.8 7.4 %fusion.2 = (f32[1024]{0:T(1024)S(1)}, f32[2048]{0:T(1024)S(1)}, f32[1024]{0:T(1024)S(1)}, f32[2048]{0:T(1024)S(1)}, bf16[1024,2048]{1,0:T(8,128)(2,1)}) fusion(f32[2048]{0:T(1024)S(1)} %bitcast.90, bf16[1024,512]{1,0:T(8,128)(2,1)S(1)} %add_convert_fusion.1, bf16[1024,512]{1,0:T(8,128)(2,1)S(1)} %copy-done.4, bf16[1024,512]{1,0:T(8,128)(2,1)S(1)} %get-tuple-element.42, ...), kind=kOutput, calls=%fused_computation.8 | convolution fusion | flops 2176837632 | bytes 11575296 | tf_op jit(solution)/shard_map/dot_general | solution.py:25
  127.2 6.4 %copy.24 = bf16[1024,2048]{0,1:T(8,128)(2,1)} copy(bf16[1024,2048]{1,0:T(8,128)(2,1)} %get-tuple-element.53) | data formatting | bytes 8388608
  133.6 1.2 copy-done.14
  134.8 4.7 %fusion.11 = bf16[512,2048]{1,0:T(8,128)(2,1)S(1)} fusion(bf16[1024,512]{1,0:T(8,128)(2,1)S(1)} %copy-done.14, bf16[1024,2048]{1,0:T(8,128)(2,1)} %all-gather.2.cloned.1.call-done, bf16[1024]{0:T(1024)(128)(2,1)S(1)} %convert_element_type.140), kind=kOutput, calls=%fused_computation.23 | convolution fusion | flops 2150629376 | bytes 7342080 | tf_op jit(solution)/shard_map/dot_general | solution.py:19
  139.7 1.0 copy-done.16
  140.7 5.0 %convolution_convert_fusion.2 = bf16[2048,512]{1,0:T(8,128)(2,1)S(1)} fusion(bf16[1024,512]{1,0:T(8,128)(2,1)S(1)} %copy-done.16, f32[2048]{0:T(1024)S(1)} %bitcast.93, f32[2048]{0:T(1024)S(1)} %bitcast.91, f32[1024]{0:T(1024)S(1)} %add_rsqrt_fusion, f32[1024]{0:T(1024)S(1)} %broadcast_multiply_fusion, bf16[1032,16,128]{2,0,1:T(8,128)(2,1)} %all-to-all-done), kind=kOutput, calls=%fused_computation.22 | convolution fusion | flops 2161115136 | bytes 7364608 | tf_op jit(solution)/shard_map/dot_general | solution.py:19
  145.8 1.3 copy-done
  147.1 1.0 constant_dynamic-slice_fusion.3
  148.1 2.8 convert_add_fusion
  150.9 0.2 collective-permute-done.2
  151.1 2.5 convert_add_fusion.1
  153.6 40.1 %reduce-scatter.5.cloned.1.call-done = bf16[128,1024]{1,0:T(8,128)(2,1)} async-done(((bf16[2048,1024]{1,0:T(8,128)(2,1)}), bf16[128,1024]{1,0:T(8,128)(2,1)}) %reduce-scatter.5.cloned.1.call-update) | async-done | bytes 262160 | tf_op jit(solution)/shard_map/reduce_scatter | solution.py:101
  193.7 1.0 convert_bitcast_fusion.1
  194.7 4.3 %all-to-all-start.1 = ((bf16[4,256,512]{2,1,0:T(8,128)(2,1)}), bf16[4,256,512]{2,1,0:T(8,128)(2,1)S(1)}, u32[]{:S(2)}, u32[]{:S(2)}) async-start(bf16[4,256,512]{2,1,0:T(8,128)(2,1)} %bitcast.5), calls=%async_computation.2 | async-start | bytes 2097152 | tf_op jit(solution)/shard_map/all_to_all | solution.py:49
  199.1 1.3 collective-permute-start.4
  200.4 2.6 collective-permute-done.4
  203.0 2.7 collective-permute-start.5
  205.8 6.8 %all-to-all-done.1 = bf16[4,256,512]{2,1,0:T(8,128)(2,1)S(1)} async-done(((bf16[4,256,512]{2,1,0:T(8,128)(2,1)}), bf16[4,256,512]{2,1,0:T(8,128)(2,1)S(1)}, u32[]{:S(2)}, u32[]{:S(2)}) %all-to-all-start.1) | async-done | bytes 1048608 | tf_op jit(solution)/shard_map/all_to_all | solution.py:49
  212.6 3.5 %all-to-all-start.3 = ((bf16[4,128,1024]{2,1,0:T(8,128)(2,1)}), bf16[4,128,1024]{2,1,0:T(8,128)(2,1)S(1)}, u32[]{:S(2)}, u32[]{:S(2)}) async-start(bf16[4,128,1024]{2,1,0:T(8,128)(2,1)} %bitcast.7), calls=%async_computation.4 | async-start | bytes 2097152 | tf_op jit(solution)/shard_map/all_to_all | solution.py:49
  216.1 1.6 collective-permute-start.6
  217.7 2.6 collective-permute-done.6
  220.3 2.7 collective-permute-start.7
  223.0 2.9 %collective-permute-done.7 = f32[2,3072]{1,0:T(2,128)S(1)} collective-permute-done((f32[2,3072]{1,0:T(2,128)S(1)}, f32[2,3072]{1,0:T(2,128)S(1)}, u32[]{:S(2)}, u32[]{:S(2)}) %collective-permute-start.7) | collective-permute-done | bytes 24608 | tf_op jit(solution)/shard_map/ppermute | solution.py:61
  226.3 0.9 collective-permute-done.8
  227.2 2.4 collective-permute-start.9
  229.6 0.2 reduce_sum.80
  229.9 1.1 broadcast_in_dim.13
  230.9 4.2 %all-to-all-start.2 = ((bf16[4,256,512]{2,1,0:T(8,128)(2,1)}), bf16[4,256,512]{2,1,0:T(8,128)(2,1)S(1)}, u32[]{:S(2)}, u32[]{:S(2)}) async-start(bf16[4,256,512]{2,1,0:T(8,128)(2,1)} %broadcast_in_dim.13), calls=%async_computation.3 | async-start | bytes 2097152 | tf_op jit(solution)/shard_map/all_to_all | solution.py:53
  235.1 5.5 %fusion.6 = f32[1024,2048]{1,0:T(8,128)} fusion(f32[1024]{0:T(1024)S(1)} %add_rsqrt_fusion, f32[1024]{0:T(1024)S(1)} %broadcast_multiply_fusion, bf16[1032,16,128]{2,0,1:T(8,128)(2,1)} %all-to-all-done), kind=kLoop, calls=%fused_computation.13 | loop fusion | flops 6291456 | bytes 12591104 | tf_op jit(solution)/shard_map/mul | solution.py:91
  240.6 3.6 %collective-permute-start.10 = (f32[2,2048]{1,0:T(2,128)S(1)}, f32[2,2048]{1,0:T(2,128)S(1)}, u32[]{:S(2)}, u32[]{:S(2)}) collective-permute-start(f32[2,2048]{1,0:T(2,128)S(1)} %add.85), channel_id=1, source_target_pairs={{0,64},{32,96},{64,0},{96,32},{1,65},{33,97},{65,1},{97,33},{2,66}... | collective-permute-start | bytes 49160 | tf_op jit(solution)/shard_map/ppermute | solution.py:61
  244.3 6.4 %collective-permute-done.10 = f32[2,2048]{1,0:T(2,128)S(1)} collective-permute-done((f32[2,2048]{1,0:T(2,128)S(1)}, f32[2,2048]{1,0:T(2,128)S(1)}, u32[]{:S(2)}, u32[]{:S(2)}) %collective-permute-start.10) | collective-permute-done | bytes 16416 | tf_op jit(solution)/shard_map/ppermute | solution.py:61
  250.8 1.1 broadcast_in_dim.14
  251.9 3.5 %all-to-all-start.4 = ((bf16[4,128,1024]{2,1,0:T(8,128)(2,1)}), bf16[4,128,1024]{2,1,0:T(8,128)(2,1)S(1)}, u32[]{:S(2)}, u32[]{:S(2)}) async-start(bf16[4,128,1024]{2,1,0:T(8,128)(2,1)} %broadcast_in_dim.14), calls=%async_computation.5 | async-start | bytes 2097152 | tf_op jit(solution)/shard_map/all_to_all | solution.py:53
  255.5 0.5 fusion.25
  256.1 0.8 copy.23
  256.9 0.3 mul.187
  257.3 1.8 bitcast_multiply_fusion.1
  259.0 10.7 %all-to-all-done.4 = bf16[4,128,1024]{2,1,0:T(8,128)(2,1)S(1)} async-done(((bf16[4,128,1024]{2,1,0:T(8,128)(2,1)}), bf16[4,128,1024]{2,1,0:T(8,128)(2,1)S(1)}, u32[]{:S(2)}, u32[]{:S(2)}) %all-to-all-start.4) | async-done | bytes 1048608 | tf_op jit(solution)/shard_map/all_to_all | solution.py:53
  269.7 0.2 mul.190
  269.9 2.1 bitcast_multiply_fusion
  272.0 2.5 reduce-scatter.7.cloned.1.call-done
  274.5 1.1 copy.25
  275.7 2.4 add_convert_fusion.4
  (70 shorter events, 1.8 us)
Async XLA Ops:
  11.4 9.1 %copy-start.10 = (s32[8,4]{0,1:T(4,128)S(1)}, s32[8,4]{0,1:T(4,128)}, u32[]{:S(2)}) copy-start(s32[8,4]{0,1:T(4,128)} %param.16) | copy-start | bytes 388
  11.4 9.6 %copy-start.2 = (bf16[1024,512]{1,0:T(8,128)(2,1)S(1)}, bf16[1024,512]{1,0:T(8,128)(2,1)}, u32[]{:S(2)}) copy-start(bf16[1024,512]{1,0:T(8,128)(2,1)} %param.14) | copy-start | bytes 3145732
  11.4 74.8 %all-to-all-start = ((bf16[1032,16,128]{2,0,1:T(8,128)(2,1)}), bf16[1032,16,128]{2,0,1:T(8,128)(2,1)}, u32[]{:S(2)}, u32[]{:S(2)}) async-start(bf16[1032,16,128]{2,0,1:T(8,128)(2,1)} %tile.2), calls=%async_computation | async-start | bytes 8454144 | tf_op jit(solution)/shard_map/all_to_all | solution.py:74
  19.7 93.4 %all-gather.2.cloned.1.call-start = ((), (), s32[]{:S(2)}) async-start(), calls=%async_computation.7 | async-start | bytes 4456448 | tf_op jit(solution)/shard_map/all_gather | solution.py:99
  20.5 173.2 %reduce-scatter.5.cloned.1.call-start = ((), (), s32[]{:S(2)}) async-start(), calls=%async_computation.8 | async-start | bytes 4456448 | tf_op jit(solution)/shard_map/reduce_scatter | solution.py:101
  20.6 0.7 copy-start.11
  21.0 1.2 copy-start.3
  21.2 2.9 %collective-permute-start = (bf16[1024,512]{1,0:T(8,128)(2,1)S(1)}, bf16[1024,512]{1,0:T(8,128)(2,1)}, u32[]{:S(2)}, u32[]{:S(2)}) collective-permute-start(bf16[1024,512]{1,0:T(8,128)(2,1)S(1)} %bitcast_multiply_fusion.3), channel_id=1, source_target_pairs={{0,16},{16,0},{1,17},{17,1},{2,18},{18,2},{3,19},{19,3},{4,20},{20... | collective-permute-start | bytes 3145736 | tf_op jit(solution)/shard_map/ppermute | solution.py:31
  22.3 4.0 %collective-permute-start.1 = (bf16[512,1024]{1,0:T(8,128)(2,1)S(1)}, bf16[512,1024]{1,0:T(8,128)(2,1)}, u32[]{:S(2)}, u32[]{:S(2)}) collective-permute-start(bf16[512,1024]{1,0:T(8,128)(2,1)S(1)} %bitcast_multiply_fusion.2), channel_id=1, source_target_pairs={{0,16},{16,0},{1,17},{17,1},{2,18},{18,2},{3,19},{19,3},{4,20},{20... | collective-permute-start | bytes 3145736 | tf_op jit(solution)/shard_map/ppermute | solution.py:31
  89.2 4.1 %copy-start.4 = (bf16[1024,512]{1,0:T(8,128)(2,1)S(1)}, bf16[1024,512]{1,0:T(8,128)(2,1)}, u32[]{:S(2)}) copy-start(bf16[1024,512]{1,0:T(8,128)(2,1)} %get-tuple-element.43) | copy-start | bytes 3145732
  93.3 11.0 %copy-start.5 = (bf16[512,1024]{1,0:T(8,128)(2,1)S(1)}, bf16[512,1024]{1,0:T(8,128)(2,1)}, u32[]{:S(2)}) copy-start(bf16[512,1024]{1,0:T(8,128)(2,1)} %get-tuple-element.40) | copy-start | bytes 3145732
  93.3 11.0 %copy-start.6 = (bf16[512,1024]{1,0:T(8,128)(2,1)S(1)}, bf16[512,1024]{1,0:T(8,128)(2,1)}, u32[]{:S(2)}) copy-start(bf16[512,1024]{1,0:T(8,128)(2,1)} %get-tuple-element.41) | copy-start | bytes 3145732
  103.3 1.0 copy-start.13
  108.7 0.7 copy-start.9
  108.7 165.8 %reduce-scatter.7.cloned.1.call-start = ((), (), s32[]{:S(2)}) async-start(), calls=%async_computation.9 | async-start | bytes 4456448
  119.8 7.4 %copy-start.15 = (bf16[1024,512]{1,0:T(8,128)(2,1)}, bf16[1024,512]{1,0:T(8,128)(2,1)S(1)}, u32[]{:S(2)}) copy-start(bf16[1024,512]{1,0:T(8,128)(2,1)S(1)} %add_convert_fusion.1) | copy-start | bytes 3145732
  133.6 1.2 copy-start.14
  139.5 1.2 copy-start.16
  139.6 8.5 %collective-permute-start.3 = (bf16[512,1024]{1,0:T(8,128)(2,1)S(1)}, bf16[512,1024]{1,0:T(8,128)(2,1)}, u32[]{:S(2)}, u32[]{:S(2)}) collective-permute-start(bf16[512,1024]{1,0:T(8,128)(2,1)S(1)} %constant_dynamic-slice_fusion.2), channel_id=1, source_target_pairs={{0,16},{16,0},{1,17},{17,1},{2,18},{18,2},{3,19},{19,3},{4,20},{20... | collective-permute-start | bytes 3145736 | tf_op jit(solution)/shard_map/ppermute | solution.py:43
  145.7 1.3 copy-start
  148.1 3.0 %collective-permute-start.2 = (bf16[1024,512]{1,0:T(8,128)(2,1)}, bf16[1024,512]{1,0:T(8,128)(2,1)}, u32[]{:S(2)}, u32[]{:S(2)}) collective-permute-start(bf16[1024,512]{1,0:T(8,128)(2,1)} %constant_dynamic-slice_fusion.3), channel_id=1, source_target_pairs={{0,16},{16,0},{1,17},{17,1},{2,18},{18,2},{3,19},{19,3},{4,20},{20... | collective-permute-start | bytes 3145736 | tf_op jit(solution)/shard_map/ppermute | solution.py:43
  148.1 3.0 %copy-start.1 = (bf16[2048,512]{1,0:T(8,128)(2,1)S(1)}, bf16[2048,512]{1,0:T(8,128)(2,1)}, u32[]{:S(2)}) copy-start(bf16[2048,512]{1,0:T(8,128)(2,1)} %copy-done) | copy-start | bytes 6291460
  194.7 31.3 %copy-start.12 = (bf16[128]{0:T(256)(128)(2,1)S(1)}, bf16[128]{0:T(256)(128)(2,1)}, u32[]{:S(2)}) copy-start(bf16[128]{0:T(256)(128)(2,1)} %param.12) | copy-start | bytes 772
  194.7 31.3 %copy-start.7 = (bf16[1024,128]{1,0:T(8,128)(2,1)S(1)}, bf16[1024,128]{1,0:T(8,128)(2,1)}, u32[]{:S(2)}) copy-start(bf16[1024,128]{1,0:T(8,128)(2,1)} %param.9) | copy-start | bytes 786436
  194.7 17.8 %all-to-all-start.1 = ((bf16[4,256,512]{2,1,0:T(8,128)(2,1)}), bf16[4,256,512]{2,1,0:T(8,128)(2,1)S(1)}, u32[]{:S(2)}, u32[]{:S(2)}) async-start(bf16[4,256,512]{2,1,0:T(8,128)(2,1)} %bitcast.5), calls=%async_computation.2 | async-start | bytes 2097152 | tf_op jit(solution)/shard_map/all_to_all | solution.py:49
  199.1 3.9 %collective-permute-start.4 = (f32[2,3072]{1,0:T(2,128)S(1)}, f32[2,3072]{1,0:T(2,128)S(1)}, u32[]{:S(2)}, u32[]{:S(2)}) collective-permute-start(f32[2,3072]{1,0:T(2,128)S(1)} %maximum_maximum_fusion), channel_id=1, source_target_pairs={{0,1},{1,0},{2,3},{3,2},{4,5},{5,4},{6,7},{7,6},{8,9},{9,8},{10,11... | collective-permute-start | bytes 73736 | tf_op jit(solution)/shard_map/ppermute | solution.py:61
  203.0 13.1 %collective-permute-start.5 = (f32[2,3072]{1,0:T(2,128)S(1)}, f32[2,3072]{1,0:T(2,128)S(1)}, u32[]{:S(2)}, u32[]{:S(2)}) collective-permute-start(f32[2,3072]{1,0:T(2,128)S(1)} %fusion.39), channel_id=1, source_target_pairs={{0,2},{1,3},{2,0},{3,1},{4,6},{5,7},{6,4},{7,5},{8,10},{9,11},{10,... | collective-permute-start | bytes 73736 | tf_op jit(solution)/shard_map/ppermute | solution.py:61
  212.6 17.3 %all-to-all-start.3 = ((bf16[4,128,1024]{2,1,0:T(8,128)(2,1)}), bf16[4,128,1024]{2,1,0:T(8,128)(2,1)S(1)}, u32[]{:S(2)}, u32[]{:S(2)}) async-start(bf16[4,128,1024]{2,1,0:T(8,128)(2,1)} %bitcast.7), calls=%async_computation.4 | async-start | bytes 2097152 | tf_op jit(solution)/shard_map/all_to_all | solution.py:49
  216.1 4.1 %collective-permute-start.6 = (f32[2,3072]{1,0:T(2,128)S(1)}, f32[2,3072]{1,0:T(2,128)S(1)}, u32[]{:S(2)}, u32[]{:S(2)}) collective-permute-start(f32[2,3072]{1,0:T(2,128)S(1)} %fusion.40), channel_id=1, source_target_pairs={{0,4},{1,5},{2,6},{3,7},{4,0},{5,1},{6,2},{7,3},{8,12},{9,13},{10,... | collective-permute-start | bytes 73736 | tf_op jit(solution)/shard_map/ppermute | solution.py:61
  220.3 5.6 %collective-permute-start.7 = (f32[2,3072]{1,0:T(2,128)S(1)}, f32[2,3072]{1,0:T(2,128)S(1)}, u32[]{:S(2)}, u32[]{:S(2)}) collective-permute-start(f32[2,3072]{1,0:T(2,128)S(1)} %add.80), channel_id=1, source_target_pairs={{0,8},{1,9},{2,10},{3,11},{4,12},{5,13},{6,14},{7,15},{8,0},{9,1},... | collective-permute-start | bytes 73736 | tf_op jit(solution)/shard_map/ppermute | solution.py:61
  225.9 1.3 collective-permute-start.8
  227.2 13.4 %collective-permute-start.9 = (f32[2,2048]{1,0:T(2,128)S(1)}, f32[2,2048]{1,0:T(2,128)S(1)}, u32[]{:S(2)}, u32[]{:S(2)}) collective-permute-start(f32[2,2048]{1,0:T(2,128)S(1)} %slice_add_fusion), channel_id=1, source_target_pairs={{0,32},{32,0},{64,96},{96,64},{1,33},{33,1},{65,97},{97,65},{2,34}... | collective-permute-start | bytes 49160 | tf_op jit(solution)/shard_map/ppermute | solution.py:61
  230.9 19.9 %all-to-all-start.2 = ((bf16[4,256,512]{2,1,0:T(8,128)(2,1)}), bf16[4,256,512]{2,1,0:T(8,128)(2,1)S(1)}, u32[]{:S(2)}, u32[]{:S(2)}) async-start(bf16[4,256,512]{2,1,0:T(8,128)(2,1)} %broadcast_in_dim.13), calls=%async_computation.3 | async-start | bytes 2097152 | tf_op jit(solution)/shard_map/all_to_all | solution.py:53
  240.6 10.0 %collective-permute-start.10 = (f32[2,2048]{1,0:T(2,128)S(1)}, f32[2,2048]{1,0:T(2,128)S(1)}, u32[]{:S(2)}, u32[]{:S(2)}) collective-permute-start(f32[2,2048]{1,0:T(2,128)S(1)} %add.85), channel_id=1, source_target_pairs={{0,64},{32,96},{64,0},{96,32},{1,65},{33,97},{65,1},{97,33},{2,66}... | collective-permute-start | bytes 49160 | tf_op jit(solution)/shard_map/ppermute | solution.py:61
  251.9 17.7 %all-to-all-start.4 = ((bf16[4,128,1024]{2,1,0:T(8,128)(2,1)}), bf16[4,128,1024]{2,1,0:T(8,128)(2,1)S(1)}, u32[]{:S(2)}, u32[]{:S(2)}) async-start(bf16[4,128,1024]{2,1,0:T(8,128)(2,1)} %broadcast_in_dim.14), calls=%async_computation.5 | async-start | bytes 2097152 | tf_op jit(solution)/shard_map/all_to_all | solution.py:53
  269.9 5.8 %copy-start.8 = (bf16[1024,128]{1,0:T(8,128)(2,1)S(1)}, bf16[1024,128]{1,0:T(8,128)(2,1)}, u32[]{:S(2)}) copy-start(bf16[1024,128]{1,0:T(8,128)(2,1)} %param.10) | copy-start | bytes 786436
Sparse Core Ops, SparseCore 0:
  22.7 90.3 all-gather.1
  116.4 77.2 reduce-scatter.4
  197.4 77.0 reduce-scatter.6
where the time goes:
time: 286 us; the launch traced here: 285 us
  waiting for transfers between devices  139 us (49%)
  starting transfers between devices  38.8 us (14%)
  matrix products  38.1 us (13%)
  other arithmetic  31 us (11%)
  local copies, waits for them, and re-layouts  23.6 us (8%)
  between operations  14.2 us (5%)
    all_to_all x1, waiting for transfers between devices, on_device(): lax.all_to_all(jnp.tile(stacked, (1, sizes['tp'])), 'tp', split_axis=1, c...  57.2 us
    reduce_scatter x1, waiting for transfers between devices, on_device(): lax.psum_scatter(partial_out, 'tp', scatter_dimension=0, tiled=True)  40.1 us
    ppermute x7, waiting for transfers between devices, butterfly_sum(): values = values + lax.ppermute(values, axis, perm=perm)  15.4 us
    ppermute x7, starting transfers between devices, butterfly_sum(): values = values + lax.ppermute(values, axis, perm=perm)  14.4 us
    unnamed x38, local copies, waits for them, and re-layouts  14.3 us
    dot_general x2, matrix products, contract_cols(): lax.dot_general(left, right, (((1,), (1,)), ((), ())), preferred_element_...  14.1 us
    all_to_all x2, waiting for transfers between devices, rows_allreduce(): lax.all_to_all(copies, axis, split_axis=0, concat_axis=0, tiled=True)  10.7 us
    dot_general x1, matrix products, on_device(): hidden = jnp.dot(scaled, full_in, preferred_element_type=jnp.float32)  9.98 us
  transfers between devices with their start and end apart: 19, of which 13 were waited for; matrix products, arithmetic and copies ran while one was open for 28% of the time, Pallas kernels for 0%

commit v1 on v0

--- a/solution.py
+++ b/solution.py
@@ -68,6 +68,7 @@
     tokens, cotangent, frame_mask, ln_gain, ln_bias, weight_in, weight_out, blocks_in, blocks_out
 ):
     frames = tokens.shape[0]
+    own_width = tokens.shape[1]
     stacked = jnp.concatenate(
         [tokens, ln_gain[None], ln_bias[None], jnp.zeros((6, tokens.shape[1]), tokens.dtype)]
     )
@@ -81,7 +82,6 @@
     full_in = pair_gather(masked_in, 0)
     full_out = pair_gather(masked_out, 1)
     width = whole_rows.shape[1]
-    own_width = tokens.shape[1]
     col_start = lax.axis_index("tp") * own_width
     gelu_exact = partial(jax.nn.gelu, approximate=False)
     values = whole_rows.astype(jnp.float32)
@@ -98,9 +98,15 @@
     ).astype(jnp.bfloat16)
     whole_grad = lax.all_gather(cotangent, "tp", axis=1, tiled=True)
     unused, whole_grad = lax.optimization_barrier((partial_out, whole_grad))
-    branch = lax.psum_scatter(
-        partial_out, "tp", scatter_dimension=0, tiled=True
-    ).astype(jnp.float32).T
+    half = frames // 2
+    first_half = lax.psum_scatter(
+        partial_out[:, :half], "tp", scatter_dimension=0, tiled=True
+    ).astype(jnp.float32)
+    received = lax.all_to_all(partial_out[:, half:], "tp", split_axis=0, concat_axis=0, tiled=True)
+    second_half = jnp.sum(
+        received.reshape(sizes["tp"], own_width, -1).astype(jnp.float32), axis=0
+    )
+    branch = jnp.concatenate([first_half, second_half], axis=1).T
     flags = frame_mask[:, None].astype(jnp.bfloat16)
     chosen = whole_grad * flags
     chosen_own = cotangent * flags

time: 286 us -> 302 us (1.056)
  waiting for transfers between devices: 139 us -> 153 us
  starting transfers between devices: 38.8 us -> 42.1 us
    all_to_all x0 -> x1, waiting for transfers between devices: none -> 19.5 us  [on_device(): lax.all_to_all(partial_out[:, half:], 'tp', split_axis=0, concat_axis=0,...]
    all_to_all x0 -> x1, starting transfers between devices: none -> 5.15 us  [on_device(): lax.all_to_all(partial_out[:, half:], 'tp', split_axis=0, concat_axis=0,...]
    reduce_scatter x1, waiting for transfers between devices: 40.1 us -> 36 us  [on_device(): lax.psum_scatter(partial_out[:, :half], 'tp', scatter_dimension=0, tiled=...]
    unnamed x38 -> x40, local copies, waits for them, and re-layouts: 14.3 us -> 11.1 us
  transfers between devices with their start and end apart: 19 -> 20, of which waited for: 13 -> 12; matrix products, arithmetic and copies ran while one was open for 28% -> 27% of each run, Pallas kernels for 0% -> 0%
where the time goes in v1:
time: 302 us; the launch traced here: 301 us
  waiting for transfers between devices  153 us (51%)
  starting transfers between devices  42.1 us (14%)
  matrix products  36.1 us (12%)
  other arithmetic  31.5 us (10%)
  local copies, waits for them, and re-layouts  23.9 us (8%)
  between operations  14.2 us (5%)
    all_to_all x1, waiting for transfers between devices, on_device(): lax.all_to_all(jnp.tile(stacked, (1, sizes['tp'])), 'tp', split_axis=1, c...  57.2 us
    reduce_scatter x1, waiting for transfers between devices, on_device(): lax.psum_scatter(partial_out[:, :half], 'tp', scatter_dimension=0, tiled=...  36 us
    all_to_all x1, waiting for transfers between devices, on_device(): lax.all_to_all(partial_out[:, half:], 'tp', split_axis=0, concat_axis=0,...  19.5 us
    ppermute x7, waiting for transfers between devices, butterfly_sum(): values = values + lax.ppermute(values, axis, perm=perm)  16.8 us
    dot_general x2, matrix products, contract_cols(): lax.dot_general(left, right, (((1,), (1,)), ((), ())), preferred_element_...  14 us
    ppermute x7, starting transfers between devices, butterfly_sum(): values = values + lax.ppermute(values, axis, perm=perm)  13 us
    unnamed x40, local copies, waits for them, and re-layouts  11.1 us
    all_to_all x2, waiting for transfers between devices, rows_allreduce(): lax.all_to_all(copies, axis, split_axis=0, concat_axis=0, tiled=True)  10.7 us
  transfers between devices with their start and end apart: 20, of which 12 were waited for; matrix products, arithmetic and copies ran while one was open for 27% of the time, Pallas kernels for 0%

profile of v1, /device:TPU:0, one launch (start us, length us, event | category | flops | bytes accessed | tf_op | source)
XLA Modules:
  0.0 300.8 jit_solution(6729428327861793396)
XLA Ops:
  7.2 1.7 concatenate.15
  8.9 2.5 tile.2
  11.4 8.3 %all-to-all-start = ((bf16[1032,16,128]{2,0,1:T(8,128)(2,1)}), bf16[1032,16,128]{2,0,1:T(8,128)(2,1)}, u32[]{:S(2)}, u32[]{:S(2)}) async-start(bf16[1032,16,128]{2,0,1:T(8,128)(2,1)} %tile.2), calls=%async_computation | async-start | bytes 8454144 | tf_op jit(solution)/shard_map/all_to_all | solution.py:75
  19.8 0.7 all-gather.2.cloned.1.call-update
  20.6 0.3 mul.164
  21.3 0.2 mul.168
  21.5 0.7 copy-done.4
  22.4 1.6 collective-permute-done
  24.0 2.3 broadcast_select_fusion.3
  26.4 2.7 broadcast_select_fusion.1
  29.0 57.2 %all-to-all-done = bf16[1032,16,128]{2,0,1:T(8,128)(2,1)} async-done(((bf16[1032,16,128]{2,0,1:T(8,128)(2,1)}), bf16[1032,16,128]{2,0,1:T(8,128)(2,1)}, u32[]{:S(2)}, u32[]{:S(2)}) %all-to-all-start) | async-done | bytes 4227104 | tf_op jit(solution)/shard_map/all_to_all | solution.py:75
  86.2 3.0 convert_reduce_fusion
  89.2 3.2 %fusion.5 = f32[1024]{0:T(1024)S(1)} fusion(f32[1024]{0:T(1024)S(1)} %broadcast_multiply_fusion, bf16[1032,16,128]{2,0,1:T(8,128)(2,1)} %all-to-all-done), kind=kLoop, calls=%fused_computation.11 | loop fusion | flops 8387584 | bytes 4202496 | tf_op jit(solution)/shard_map/reduce_sum | solution.py:90
  92.4 0.8 slice_convert_fusion.1
  93.3 10.0 %multiply_convert_fusion = (bf16[1024,512]{1,0:T(8,128)(2,1)S(1)}, f32[1024,512]{1,0:T(8,128)}, f32[1024,512]{1,0:T(8,128)}) fusion(bf16[1024,512]{1,0:T(8,128)(2,1)S(1)} %copy-done.5, bf16[1024,512]{1,0:T(8,128)(2,1)S(1)} %get-tuple-element.44, f32[2048]{0:T(1024)S(1)} %bitcast.94, f32[2048]{0:T(1024)S(1)} %bitcast.91, f32[1024]{0:T(1024)S(1)} %add_rsqrt_fusion, ...), kind=kOutput, calls=%fused_computation.35 | convolution fusion | flops 2198339584 | bytes 11558912 | tf_op jit(solution)/shard_map/dot_general | solution.py:94
  103.3 2.4 convolution_convert_fusion.1
  105.7 2.4 fusion.32
  108.1 0.2 reduce-scatter.7.cloned.1.call-start
  108.4 0.4 copy-done.10
  108.8 4.3 %all-gather.2.cloned.1.call-done = bf16[1024,2048]{1,0:T(8,128)(2,1)} async-done(((bf16[1024,128]{1,0:T(8,128)(2,1)}), bf16[1024,2048]{1,0:T(8,128)(2,1)}) %all-gather.2.cloned.1.call-update) | async-done | bytes 4194320 | tf_op jit(solution)/shard_map/all_gather | solution.py:99
  113.1 6.7 %add_convert_fusion.1 = bf16[1024,512]{1,0:T(8,128)(2,1)S(1)} fusion(f32[1024,512]{1,0:T(8,128)} %get-tuple-element.37, f32[1024,512]{1,0:T(8,128)} %get-tuple-element.54, bf16[1024,2048]{1,0:T(8,128)(2,1)} %all-gather.2.cloned.1.call-done, bf16[1024]{0:T(1024)(128)(2,1)S(1)} %convert_element_type.145, bf16[512,1024]{1,0:T(8,128)(2,1)} %get-tuple-element.43, ...), kind=kOutput, calls=%fused_computation.32 | convolution fusion | flops 2161115136 | bytes 11536384 | tf_op jit(solution)/shard_map/dot_general | solution.py:25
  119.8 7.3 %fusion.2 = (f32[1024]{0:T(1024)S(1)}, f32[2048]{0:T(1024)S(1)}, f32[1024]{0:T(1024)S(1)}, f32[2048]{0:T(1024)S(1)}, bf16[1024,2048]{1,0:T(8,128)(2,1)}) fusion(f32[2048]{0:T(1024)S(1)} %bitcast.92, bf16[1024,512]{1,0:T(8,128)(2,1)S(1)} %add_convert_fusion.1, bf16[1024,512]{1,0:T(8,128)(2,1)S(1)} %copy-done.5, bf16[1024,512]{1,0:T(8,128)(2,1)S(1)} %get-tuple-element.44, ...), kind=kOutput, calls=%fused_computation.8 | convolution fusion | flops 2176837632 | bytes 11575296 | tf_op jit(solution)/shard_map/dot_general | solution.py:25
  127.1 6.4 %copy.24 = bf16[1024,2048]{0,1:T(8,128)(2,1)} copy(bf16[1024,2048]{1,0:T(8,128)(2,1)} %get-tuple-element.55) | data formatting | bytes 8388608
  133.5 5.1 %all-to-all-start.1 = ((bf16[16,128,512]{2,1,0:T(8,128)(2,1)}), bf16[16,128,512]{2,1,0:T(8,128)(2,1)S(1)}, u32[]{:S(2)}, u32[]{:S(2)}) async-start(bf16[16,128,512]{2,1,0:T(8,128)(2,1)} %bitcast.73), calls=%async_computation.2 | async-start | bytes 4194304 | tf_op jit(solution)/shard_map/all_to_all | solution.py:105
  138.6 4.6 %fusion.11 = bf16[512,2048]{1,0:T(8,128)(2,1)S(1)} fusion(bf16[1024,512]{1,0:T(8,128)(2,1)S(1)} %copy-done.15, bf16[1024,2048]{1,0:T(8,128)(2,1)} %all-gather.2.cloned.1.call-done, bf16[1024]{0:T(1024)(128)(2,1)S(1)} %convert_element_type.145), kind=kOutput, calls=%fused_computation.24 | convolution fusion | flops 2150629376 | bytes 7342080 | tf_op jit(solution)/shard_map/dot_general | solution.py:19
  143.3 1.1 constant_dynamic-slice_fusion.2
  144.4 0.9 copy-done.17
  145.3 5.0 %convolution_convert_fusion.2 = bf16[2048,512]{1,0:T(8,128)(2,1)S(1)} fusion(bf16[1024,512]{1,0:T(8,128)(2,1)S(1)} %copy-done.17, f32[2048]{0:T(1024)S(1)} %bitcast.95, f32[2048]{0:T(1024)S(1)} %bitcast.93, f32[1024]{0:T(1024)S(1)} %add_rsqrt_fusion, f32[1024]{0:T(1024)S(1)} %broadcast_multiply_fusion, bf16[1032,16,128]{2,0,1:T(8,128)(2,1)} %all-to-all-done), kind=kOutput, calls=%fused_computation.23 | convolution fusion | flops 2161115136 | bytes 7364608 | tf_op jit(solution)/shard_map/dot_general | solution.py:19
  150.4 1.2 constant_dynamic-slice_fusion.3
  151.5 0.5 copy-done.1
  152.0 19.5 %all-to-all-done.1 = bf16[16,128,512]{2,1,0:T(8,128)(2,1)S(1)} async-done(((bf16[16,128,512]{2,1,0:T(8,128)(2,1)}), bf16[16,128,512]{2,1,0:T(8,128)(2,1)S(1)}, u32[]{:S(2)}, u32[]{:S(2)}) %all-to-all-start.1) | async-done | bytes 2097184 | tf_op jit(solution)/shard_map/all_to_all | solution.py:105
  171.5 0.3 convert_reduce_fusion.2
  171.8 36.0 %reduce-scatter.5.cloned.1.call-done = bf16[128,512]{1,0:T(8,128)(2,1)} async-done(((bf16[2048,512]{1,0:T(8,128)(2,1)}), bf16[128,512]{1,0:T(8,128)(2,1)}) %reduce-scatter.5.cloned.1.call-update) | async-done | bytes 131088 | tf_op jit(solution)/shard_map/reduce_scatter | solution.py:102
  207.8 0.9 convert_element_type.153
  208.7 3.0 %convert_add_fusion = bf16[512,1024]{1,0:T(8,128)(2,1)} fusion(bf16[512,1024]{1,0:T(8,128)(2,1)} %collective-permute-done.3, bf16[512,2048]{1,0:T(8,128)(2,1)} %copy-done, s32[]{:T(128)S(6)} %select_n.43), kind=kLoop, calls=%fused_computation.30 | loop fusion | flops 2097152 | bytes 3145732 | tf_op jit(solution)/shard_map/add | solution.py:44
  211.8 2.5 convert_add_fusion.1
  214.3 4.4 %all-to-all-start.2 = ((bf16[4,256,512]{2,1,0:T(8,128)(2,1)}), bf16[4,256,512]{2,1,0:T(8,128)(2,1)S(1)}, u32[]{:S(2)}, u32[]{:S(2)}) async-start(bf16[4,256,512]{2,1,0:T(8,128)(2,1)} %bitcast.6), calls=%async_computation.3 | async-start | bytes 2097152 | tf_op jit(solution)/shard_map/all_to_all | solution.py:49
  218.7 1.4 collective-permute-start.4
  220.1 3.0 %collective-permute-done.4 = f32[2,3072]{1,0:T(2,128)S(1)} collective-permute-done((f32[2,3072]{1,0:T(2,128)S(1)}, f32[2,3072]{1,0:T(2,128)S(1)}, u32[]{:S(2)}, u32[]{:S(2)}) %collective-permute-start.4) | collective-permute-done | bytes 24608 | tf_op jit(solution)/shard_map/ppermute | solution.py:61
  223.2 2.7 collective-permute-start.5
  225.9 6.3 %all-to-all-done.2 = bf16[4,256,512]{2,1,0:T(8,128)(2,1)S(1)} async-done(((bf16[4,256,512]{2,1,0:T(8,128)(2,1)}), bf16[4,256,512]{2,1,0:T(8,128)(2,1)S(1)}, u32[]{:S(2)}, u32[]{:S(2)}) %all-to-all-start.2) | async-done | bytes 1048608 | tf_op jit(solution)/shard_map/all_to_all | solution.py:49
  232.1 3.5 %all-to-all-start.4 = ((bf16[4,128,1024]{2,1,0:T(8,128)(2,1)}), bf16[4,128,1024]{2,1,0:T(8,128)(2,1)S(1)}, u32[]{:S(2)}, u32[]{:S(2)}) async-start(bf16[4,128,1024]{2,1,0:T(8,128)(2,1)} %bitcast.8), calls=%async_computation.5 | async-start | bytes 2097152 | tf_op jit(solution)/shard_map/all_to_all | solution.py:49
  235.7 0.8 collective-permute-start.6
  236.6 3.3 %collective-permute-done.6 = f32[2,3072]{1,0:T(2,128)S(1)} collective-permute-done((f32[2,3072]{1,0:T(2,128)S(1)}, f32[2,3072]{1,0:T(2,128)S(1)}, u32[]{:S(2)}, u32[]{:S(2)}) %collective-permute-start.6) | collective-permute-done | bytes 24608 | tf_op jit(solution)/shard_map/ppermute | solution.py:61
  239.9 2.2 collective-permute-start.7
  242.1 3.2 %collective-permute-done.7 = f32[2,3072]{1,0:T(2,128)S(1)} collective-permute-done((f32[2,3072]{1,0:T(2,128)S(1)}, f32[2,3072]{1,0:T(2,128)S(1)}, u32[]{:S(2)}, u32[]{:S(2)}) %collective-permute-start.7) | collective-permute-done | bytes 24608 | tf_op jit(solution)/shard_map/ppermute | solution.py:61
  245.7 0.9 collective-permute-done.8
  246.6 2.1 collective-permute-start.9
  248.7 0.2 reduce_sum.90
  249.0 1.1 broadcast_in_dim.13
  250.0 3.7 %all-to-all-start.3 = ((bf16[4,256,512]{2,1,0:T(8,128)(2,1)}), bf16[4,256,512]{2,1,0:T(8,128)(2,1)S(1)}, u32[]{:S(2)}, u32[]{:S(2)}) async-start(bf16[4,256,512]{2,1,0:T(8,128)(2,1)} %broadcast_in_dim.13), calls=%async_computation.4 | async-start | bytes 2097152 | tf_op jit(solution)/shard_map/all_to_all | solution.py:53
  253.7 5.5 %fusion.6 = f32[1024,2048]{1,0:T(8,128)} fusion(f32[1024]{0:T(1024)S(1)} %add_rsqrt_fusion, f32[1024]{0:T(1024)S(1)} %broadcast_multiply_fusion, bf16[1032,16,128]{2,0,1:T(8,128)(2,1)} %all-to-all-done), kind=kLoop, calls=%fused_computation.13 | loop fusion | flops 6291456 | bytes 12591104 | tf_op jit(solution)/shard_map/mul | solution.py:91
  259.2 3.7 %collective-permute-start.10 = (f32[2,2048]{1,0:T(2,128)S(1)}, f32[2,2048]{1,0:T(2,128)S(1)}, u32[]{:S(2)}, u32[]{:S(2)}) collective-permute-start(f32[2,2048]{1,0:T(2,128)S(1)} %add.85), channel_id=1, source_target_pairs={{0,64},{32,96},{64,0},{96,32},{1,65},{33,97},{65,1},{97,33},{2,66}... | collective-permute-start | bytes 49160 | tf_op jit(solution)/shard_map/ppermute | solution.py:61
  262.9 6.4 %collective-permute-done.10 = f32[2,2048]{1,0:T(2,128)S(1)} collective-permute-done((f32[2,2048]{1,0:T(2,128)S(1)}, f32[2,2048]{1,0:T(2,128)S(1)}, u32[]{:S(2)}, u32[]{:S(2)}) %collective-permute-start.10) | collective-permute-done | bytes 16416 | tf_op jit(solution)/shard_map/ppermute | solution.py:61
  269.5 1.1 broadcast_in_dim.14
  270.6 3.5 %all-to-all-start.5 = ((bf16[4,128,1024]{2,1,0:T(8,128)(2,1)}), bf16[4,128,1024]{2,1,0:T(8,128)(2,1)S(1)}, u32[]{:S(2)}, u32[]{:S(2)}) async-start(bf16[4,128,1024]{2,1,0:T(8,128)(2,1)} %broadcast_in_dim.14), calls=%async_computation.6 | async-start | bytes 2097152 | tf_op jit(solution)/shard_map/all_to_all | solution.py:53
  274.2 0.5 fusion.25
  274.8 0.8 copy.23
  275.6 0.3 mul.187
  275.9 1.8 bitcast_multiply_fusion.1
  277.7 10.7 %all-to-all-done.5 = bf16[4,128,1024]{2,1,0:T(8,128)(2,1)S(1)} async-done(((bf16[4,128,1024]{2,1,0:T(8,128)(2,1)}), bf16[4,128,1024]{2,1,0:T(8,128)(2,1)S(1)}, u32[]{:S(2)}, u32[]{:S(2)}) %all-to-all-start.5) | async-done | bytes 1048608 | tf_op jit(solution)/shard_map/all_to_all | solution.py:53
  288.7 2.1 bitcast_multiply_fusion
  290.7 1.1 copy.25
  291.9 2.4 add_convert_fusion.4
  (77 shorter events, 1.9 us)
Async XLA Ops:
  11.4 9.1 %copy-start.11 = (s32[8,4]{0,1:T(4,128)S(1)}, s32[8,4]{0,1:T(4,128)}, u32[]{:S(2)}) copy-start(s32[8,4]{0,1:T(4,128)} %param.16) | copy-start | bytes 388
  11.4 9.6 %copy-start.3 = (bf16[1024,512]{1,0:T(8,128)(2,1)S(1)}, bf16[1024,512]{1,0:T(8,128)(2,1)}, u32[]{:S(2)}) copy-start(bf16[1024,512]{1,0:T(8,128)(2,1)} %param.14) | copy-start | bytes 3145732
  11.4 74.8 %all-to-all-start = ((bf16[1032,16,128]{2,0,1:T(8,128)(2,1)}), bf16[1032,16,128]{2,0,1:T(8,128)(2,1)}, u32[]{:S(2)}, u32[]{:S(2)}) async-start(bf16[1032,16,128]{2,0,1:T(8,128)(2,1)} %tile.2), calls=%async_computation | async-start | bytes 8454144 | tf_op jit(solution)/shard_map/all_to_all | solution.py:75
  19.7 93.4 %all-gather.2.cloned.1.call-start = ((), (), s32[]{:S(2)}) async-start(), calls=%async_computation.8 | async-start | bytes 4456448 | tf_op jit(solution)/shard_map/all_gather | solution.py:99
  20.4 187.3 %reduce-scatter.5.cloned.1.call-start = ((), (), s32[]{:S(2)}) async-start(), calls=%async_computation.9 | async-start | bytes 2228224 | tf_op jit(solution)/shard_map/reduce_scatter | solution.py:102
  20.6 0.7 copy-start.12
  21.0 1.2 copy-start.4
  21.1 2.9 collective-permute-start
  22.3 4.0 %collective-permute-start.1 = (bf16[512,1024]{1,0:T(8,128)(2,1)S(1)}, bf16[512,1024]{1,0:T(8,128)(2,1)}, u32[]{:S(2)}, u32[]{:S(2)}) collective-permute-start(bf16[512,1024]{1,0:T(8,128)(2,1)S(1)} %bitcast_multiply_fusion.2), channel_id=1, source_target_pairs={{0,16},{16,0},{1,17},{17,1},{2,18},{18,2},{3,19},{19,3},{4,20},{20... | collective-permute-start | bytes 3145736 | tf_op jit(solution)/shard_map/ppermute | solution.py:31
  89.2 4.1 %copy-start.5 = (bf16[1024,512]{1,0:T(8,128)(2,1)S(1)}, bf16[1024,512]{1,0:T(8,128)(2,1)}, u32[]{:S(2)}) copy-start(bf16[1024,512]{1,0:T(8,128)(2,1)} %get-tuple-element.45) | copy-start | bytes 3145732
  93.3 10.0 %copy-start.6 = (bf16[512,1024]{1,0:T(8,128)(2,1)S(1)}, bf16[512,1024]{1,0:T(8,128)(2,1)}, u32[]{:S(2)}) copy-start(bf16[512,1024]{1,0:T(8,128)(2,1)} %get-tuple-element.42) | copy-start | bytes 3145732
  93.3 10.0 %copy-start.7 = (bf16[512,1024]{1,0:T(8,128)(2,1)S(1)}, bf16[512,1024]{1,0:T(8,128)(2,1)}, u32[]{:S(2)}) copy-start(bf16[512,1024]{1,0:T(8,128)(2,1)} %get-tuple-element.43) | copy-start | bytes 3145732
  103.3 2.4 copy-start.14
  108.1 0.7 copy-start.10
  108.1 182.6 %reduce-scatter.7.cloned.1.call-start = ((), (), s32[]{:S(2)}) async-start(), calls=%async_computation.10 | async-start | bytes 4456448
  119.8 7.3 %copy-start.16 = (bf16[1024,512]{1,0:T(8,128)(2,1)}, bf16[1024,512]{1,0:T(8,128)(2,1)S(1)}, u32[]{:S(2)}) copy-start(bf16[1024,512]{1,0:T(8,128)(2,1)S(1)} %add_convert_fusion.1) | copy-start | bytes 3145732
  133.5 5.2 %copy-start.15 = (bf16[1024,512]{1,0:T(8,128)(2,1)S(1)}, bf16[1024,512]{1,0:T(8,128)(2,1)}, u32[]{:S(2)}) copy-start(bf16[1024,512]{1,0:T(8,128)(2,1)} %copy-done.14) | copy-start | bytes 3145732
  133.5 38.0 %all-to-all-start.1 = ((bf16[16,128,512]{2,1,0:T(8,128)(2,1)}), bf16[16,128,512]{2,1,0:T(8,128)(2,1)S(1)}, u32[]{:S(2)}, u32[]{:S(2)}) async-start(bf16[16,128,512]{2,1,0:T(8,128)(2,1)} %bitcast.73), calls=%async_computation.2 | async-start | bytes 4194304 | tf_op jit(solution)/shard_map/all_to_all | solution.py:105
  143.3 7.0 %copy-start = (bf16[512,2048]{1,0:T(8,128)(2,1)}, bf16[512,2048]{1,0:T(8,128)(2,1)S(1)}, u32[]{:S(2)}) copy-start(bf16[512,2048]{1,0:T(8,128)(2,1)S(1)} %fusion.11) | copy-start | bytes 6291460
  143.3 2.0 copy-start.17
  144.4 64.3 %collective-permute-start.3 = (bf16[512,1024]{1,0:T(8,128)(2,1)}, bf16[512,1024]{1,0:T(8,128)(2,1)}, u32[]{:S(2)}, u32[]{:S(2)}) collective-permute-start(bf16[512,1024]{1,0:T(8,128)(2,1)} %constant_dynamic-slice_fusion.2), channel_id=1, source_target_pairs={{0,16},{16,0},{1,17},{17,1},{2,18},{18,2},{3,19},{19,3},{4,20},{20... | collective-permute-start | bytes 3145736 | tf_op jit(solution)/shard_map/ppermute | solution.py:43
  150.4 1.7 copy-start.1
  152.0 59.8 %collective-permute-start.2 = (bf16[1024,512]{1,0:T(8,128)(2,1)}, bf16[1024,512]{1,0:T(8,128)(2,1)}, u32[]{:S(2)}, u32[]{:S(2)}) collective-permute-start(bf16[1024,512]{1,0:T(8,128)(2,1)} %constant_dynamic-slice_fusion.3), channel_id=1, source_target_pairs={{0,16},{16,0},{1,17},{17,1},{2,18},{18,2},{3,19},{19,3},{4,20},{20... | collective-permute-start | bytes 3145736 | tf_op jit(solution)/shard_map/ppermute | solution.py:43
  208.7 3.1 %copy-start.2 = (bf16[2048,512]{1,0:T(8,128)(2,1)S(1)}, bf16[2048,512]{1,0:T(8,128)(2,1)}, u32[]{:S(2)}) copy-start(bf16[2048,512]{1,0:T(8,128)(2,1)} %copy-done.1) | copy-start | bytes 6291460
  214.3 31.2 %copy-start.13 = (bf16[128]{0:T(256)(128)(2,1)S(1)}, bf16[128]{0:T(256)(128)(2,1)}, u32[]{:S(2)}) copy-start(bf16[128]{0:T(256)(128)(2,1)} %param.12) | copy-start | bytes 772
  214.3 31.2 %copy-start.8 = (bf16[1024,128]{1,0:T(8,128)(2,1)S(1)}, bf16[1024,128]{1,0:T(8,128)(2,1)}, u32[]{:S(2)}) copy-start(bf16[1024,128]{1,0:T(8,128)(2,1)} %param.9) | copy-start | bytes 786436
  214.3 17.8 %all-to-all-start.2 = ((bf16[4,256,512]{2,1,0:T(8,128)(2,1)}), bf16[4,256,512]{2,1,0:T(8,128)(2,1)S(1)}, u32[]{:S(2)}, u32[]{:S(2)}) async-start(bf16[4,256,512]{2,1,0:T(8,128)(2,1)} %bitcast.6), calls=%async_computation.3 | async-start | bytes 2097152 | tf_op jit(solution)/shard_map/all_to_all | solution.py:49
  218.7 4.5 %collective-permute-start.4 = (f32[2,3072]{1,0:T(2,128)S(1)}, f32[2,3072]{1,0:T(2,128)S(1)}, u32[]{:S(2)}, u32[]{:S(2)}) collective-permute-start(f32[2,3072]{1,0:T(2,128)S(1)} %maximum_maximum_fusion), channel_id=1, source_target_pairs={{0,1},{1,0},{2,3},{3,2},{4,5},{5,4},{6,7},{7,6},{8,9},{9,8},{10,11... | collective-permute-start | bytes 73736 | tf_op jit(solution)/shard_map/ppermute | solution.py:61
  223.2 12.5 %collective-permute-start.5 = (f32[2,3072]{1,0:T(2,128)S(1)}, f32[2,3072]{1,0:T(2,128)S(1)}, u32[]{:S(2)}, u32[]{:S(2)}) collective-permute-start(f32[2,3072]{1,0:T(2,128)S(1)} %fusion.40), channel_id=1, source_target_pairs={{0,2},{1,3},{2,0},{3,1},{4,6},{5,7},{6,4},{7,5},{8,10},{9,11},{10,... | collective-permute-start | bytes 73736 | tf_op jit(solution)/shard_map/ppermute | solution.py:61
  232.1 16.8 %all-to-all-start.4 = ((bf16[4,128,1024]{2,1,0:T(8,128)(2,1)}), bf16[4,128,1024]{2,1,0:T(8,128)(2,1)S(1)}, u32[]{:S(2)}, u32[]{:S(2)}) async-start(bf16[4,128,1024]{2,1,0:T(8,128)(2,1)} %bitcast.8), calls=%async_computation.5 | async-start | bytes 2097152 | tf_op jit(solution)/shard_map/all_to_all | solution.py:49
  235.7 4.2 %collective-permute-start.6 = (f32[2,3072]{1,0:T(2,128)S(1)}, f32[2,3072]{1,0:T(2,128)S(1)}, u32[]{:S(2)}, u32[]{:S(2)}) collective-permute-start(f32[2,3072]{1,0:T(2,128)S(1)} %fusion.41), channel_id=1, source_target_pairs={{0,4},{1,5},{2,6},{3,7},{4,0},{5,1},{6,2},{7,3},{8,12},{9,13},{10,... | collective-permute-start | bytes 73736 | tf_op jit(solution)/shard_map/ppermute | solution.py:61
  239.9 5.4 %collective-permute-start.7 = (f32[2,3072]{1,0:T(2,128)S(1)}, f32[2,3072]{1,0:T(2,128)S(1)}, u32[]{:S(2)}, u32[]{:S(2)}) collective-permute-start(f32[2,3072]{1,0:T(2,128)S(1)} %add.80), channel_id=1, source_target_pairs={{0,8},{1,9},{2,10},{3,11},{4,12},{5,13},{6,14},{7,15},{8,0},{9,1},... | collective-permute-start | bytes 73736 | tf_op jit(solution)/shard_map/ppermute | solution.py:61
  245.4 1.3 collective-permute-start.8
  246.6 12.6 %collective-permute-start.9 = (f32[2,2048]{1,0:T(2,128)S(1)}, f32[2,2048]{1,0:T(2,128)S(1)}, u32[]{:S(2)}, u32[]{:S(2)}) collective-permute-start(f32[2,2048]{1,0:T(2,128)S(1)} %slice_add_fusion), channel_id=1, source_target_pairs={{0,32},{32,0},{64,96},{96,64},{1,33},{33,1},{65,97},{97,65},{2,34}... | collective-permute-start | bytes 49160 | tf_op jit(solution)/shard_map/ppermute | solution.py:61
  250.0 19.5 %all-to-all-start.3 = ((bf16[4,256,512]{2,1,0:T(8,128)(2,1)}), bf16[4,256,512]{2,1,0:T(8,128)(2,1)S(1)}, u32[]{:S(2)}, u32[]{:S(2)}) async-start(bf16[4,256,512]{2,1,0:T(8,128)(2,1)} %broadcast_in_dim.13), calls=%async_computation.4 | async-start | bytes 2097152 | tf_op jit(solution)/shard_map/all_to_all | solution.py:53
  259.2 10.1 %collective-permute-start.10 = (f32[2,2048]{1,0:T(2,128)S(1)}, f32[2,2048]{1,0:T(2,128)S(1)}, u32[]{:S(2)}, u32[]{:S(2)}) collective-permute-start(f32[2,2048]{1,0:T(2,128)S(1)} %add.85), channel_id=1, source_target_pairs={{0,64},{32,96},{64,0},{96,32},{1,65},{33,97},{65,1},{97,33},{2,66}... | collective-permute-start | bytes 49160 | tf_op jit(solution)/shard_map/ppermute | solution.py:61
  270.6 17.8 %all-to-all-start.5 = ((bf16[4,128,1024]{2,1,0:T(8,128)(2,1)}), bf16[4,128,1024]{2,1,0:T(8,128)(2,1)S(1)}, u32[]{:S(2)}, u32[]{:S(2)}) async-start(bf16[4,128,1024]{2,1,0:T(8,128)(2,1)} %broadcast_in_dim.14), calls=%async_computation.6 | async-start | bytes 2097152 | tf_op jit(solution)/shard_map/all_to_all | solution.py:53
  288.6 3.2 %copy-start.9 = (bf16[1024,128]{1,0:T(8,128)(2,1)S(1)}, bf16[1024,128]{1,0:T(8,128)(2,1)}, u32[]{:S(2)}) copy-start(bf16[1024,128]{1,0:T(8,128)(2,1)} %param.10) | copy-start | bytes 786436
Sparse Core Ops, SparseCore 0:
  22.7 90.3 all-gather.1
  116.3 91.3 reduce-scatter.4
  211.5 77.0 reduce-scatter.6

commit v2 on v0

--- a/solution.py
+++ b/solution.py
@@ -68,6 +68,7 @@
     tokens, cotangent, frame_mask, ln_gain, ln_bias, weight_in, weight_out, blocks_in, blocks_out
 ):
     frames = tokens.shape[0]
+    own_width = tokens.shape[1]
     stacked = jnp.concatenate(
         [tokens, ln_gain[None], ln_bias[None], jnp.zeros((6, tokens.shape[1]), tokens.dtype)]
     )
@@ -81,7 +82,6 @@
     full_in = pair_gather(masked_in, 0)
     full_out = pair_gather(masked_out, 1)
     width = whole_rows.shape[1]
-    own_width = tokens.shape[1]
     col_start = lax.axis_index("tp") * own_width
     gelu_exact = partial(jax.nn.gelu, approximate=False)
     values = whole_rows.astype(jnp.float32)
@@ -96,11 +96,14 @@
     partial_out = lax.dot_general(
         full_out, active, (((0,), (1,)), ((), ())), preferred_element_type=jnp.float32
     ).astype(jnp.bfloat16)
-    whole_grad = lax.all_gather(cotangent, "tp", axis=1, tiled=True)
+    whole_grad = lax.all_to_all(
+        jnp.tile(cotangent, (1, sizes["tp"])), "tp", split_axis=1, concat_axis=1, tiled=True
+    )
     unused, whole_grad = lax.optimization_barrier((partial_out, whole_grad))
-    branch = lax.psum_scatter(
-        partial_out, "tp", scatter_dimension=0, tiled=True
-    ).astype(jnp.float32).T
+    received = lax.all_to_all(partial_out, "tp", split_axis=0, concat_axis=0, tiled=True)
+    branch = jnp.sum(
+        received.reshape(sizes["tp"], own_width, -1).astype(jnp.float32), axis=0
+    ).T
     flags = frame_mask[:, None].astype(jnp.bfloat16)
     chosen = whole_grad * flags
     chosen_own = cotangent * flags
@@ -108,9 +111,10 @@
     unused, gelu_back = jax.vjp(gelu_exact, hidden)
     back_hidden = gelu_back(back_active)[0].astype(jnp.bfloat16)
     partial_normed = contract_cols(back_hidden, full_in).astype(jnp.bfloat16)
-    back_normed = lax.psum_scatter(
-        partial_normed, "tp", scatter_dimension=1, tiled=True
-    ).astype(jnp.float32)
+    received = lax.all_to_all(partial_normed, "tp", split_axis=1, concat_axis=0, tiled=True)
+    back_normed = jnp.sum(
+        received.reshape(sizes["tp"], frames, -1).astype(jnp.float32), axis=0
+    )
     piece = partial_normed.astype(jnp.float32)
     piece_scaled = piece * gain_f
     row_sums = jnp.stack([jnp.sum(piece_scaled, axis=1), jnp.sum(piece_scaled * normed, axis=1)])

time: 286 us -> 344 us (1.20)
  waiting for transfers between devices: 139 us -> 196 us
  between operations: 14.2 us -> 1.12 us
  starting transfers between devices: 38.8 us -> 47.8 us
  other arithmetic: 31 us -> 35.7 us
    all_to_all x0 -> x3, waiting for transfers between devices: none -> 107 us  [the longest x1 38 us: on_device(): lax.all_to_all(jnp.tile(cotangent, (1, sizes['tp'])), 'tp', split_axis=1,...]
    reduce_scatter x1 -> x0, waiting for transfers between devices: 40.1 us -> none  [on_device(): lax.psum_scatter(partial_out, 'tp', scatter_dimension=0, tiled=True)]
    all_to_all x0 -> x3, starting transfers between devices: none -> 14.1 us  [the longest x1 4.86 us: on_device(): lax.all_to_all(partial_out, 'tp', split_axis=0, concat_axis=0, tiled=True)]
    all_to_all x0 -> x2, local copies, waits for them, and re-layouts: none -> 9.5 us  [the longest x1 6.4 us: on_device(): lax.all_to_all(jnp.tile(cotangent, (1, sizes['tp'])), 'tp', split_axis=1,...]
    unnamed x38, local copies, waits for them, and re-layouts: 14.3 us -> 5.13 us
    reduce_sum x0 -> x2, other arithmetic: none -> 5.96 us  [the longest x1 3.15 us: on_device(): jnp.sum(received.reshape(sizes['tp'], own_width, -1).astype(jnp.float32),...]
    ppermute x7, starting transfers between devices: 14.4 us -> 9.74 us  [butterfly_sum(): values = values + lax.ppermute(values, axis, perm=perm)]
    all_gather x1 -> x0, waiting for transfers between devices: 3.7 us -> none  [on_device(): whole_grad = lax.all_gather(cotangent, 'tp', axis=1, tiled=True)]
  transfers between devices with their start and end apart: 19 -> 19, of which waited for: 13 -> 13; matrix products, arithmetic and copies ran while one was open for 28% -> 23% of each run, Pallas kernels for 0% -> 0%
where the time goes in v2:
time: 344 us; the launch traced here: 342 us
  waiting for transfers between devices  196 us (57%)
  starting transfers between devices  47.8 us (14%)
  other arithmetic  35.7 us (10%)
  matrix products  34.7 us (10%)
  local copies, waits for them, and re-layouts  26.7 us (8%)
    all_to_all x1, waiting for transfers between devices, on_device(): lax.all_to_all(jnp.tile(stacked, (1, sizes['tp'])), 'tp', split_axis=1, c...  55.1 us
    all_to_all x1, waiting for transfers between devices, on_device(): lax.all_to_all(jnp.tile(cotangent, (1, sizes['tp'])), 'tp', split_axis=1,...  38 us
    all_to_all x1, waiting for transfers between devices, on_device(): lax.all_to_all(partial_out, 'tp', split_axis=0, concat_axis=0, tiled=True)  34.9 us
    all_to_all x1, waiting for transfers between devices, on_device(): lax.all_to_all(partial_normed, 'tp', split_axis=1, concat_axis=0, tiled=T...  34.1 us
    ppermute x7, waiting for transfers between devices, butterfly_sum(): values = values + lax.ppermute(values, axis, perm=perm)  16.7 us
    dot_general x2, matrix products, contract_cols(): lax.dot_general(left, right, (((1,), (1,)), ((), ())), preferred_element_...  12.8 us
    dot_general x1, matrix products, on_device(): hidden = jnp.dot(scaled, full_in, preferred_element_type=jnp.float32)  9.98 us
    ppermute x7, starting transfers between devices, butterfly_sum(): values = values + lax.ppermute(values, axis, perm=perm)  9.74 us
  transfers between devices with their start and end apart: 19, of which 13 were waited for; matrix products, arithmetic and copies ran while one was open for 23% of the time, Pallas kernels for 0%

profile of v2, /device:TPU:0, one launch (start us, length us, event | category | flops | bytes accessed | tf_op | source)
XLA Modules:
  0.0 342.1 jit_solution(15829873401266302079)
XLA Ops:
  0.6 1.7 concatenate.12
  2.3 2.5 tile.4
  4.9 8.3 %all-to-all-start = ((bf16[1032,16,128]{2,0,1:T(8,128)(2,1)}), bf16[1032,16,128]{2,0,1:T(8,128)(2,1)}, u32[]{:S(2)}, u32[]{:S(2)}) async-start(bf16[1032,16,128]{2,0,1:T(8,128)(2,1)} %tile.4), calls=%async_computation | async-start | bytes 8454144 | tf_op jit(solution)/shard_map/all_to_all | solution.py:75
  13.3 0.3 mul.164
  14.0 0.2 mul.168
  14.2 0.7 copy-done.4
  15.1 1.6 collective-permute-done
  16.7 2.3 broadcast_select_fusion.3
  19.0 2.8 broadcast_select_fusion.1
  21.8 55.1 %all-to-all-done = bf16[1032,16,128]{2,0,1:T(8,128)(2,1)} async-done(((bf16[1032,16,128]{2,0,1:T(8,128)(2,1)}), bf16[1032,16,128]{2,0,1:T(8,128)(2,1)}, u32[]{:S(2)}, u32[]{:S(2)}) %all-to-all-start) | async-done | bytes 4227104 | tf_op jit(solution)/shard_map/all_to_all | solution.py:75
  76.9 2.8 tile.5
  79.6 4.7 %all-to-all-start.1 = ((bf16[1024,16,128]{2,0,1:T(8,128)(2,1)}), bf16[1024,16,128]{2,0,1:T(8,128)(2,1)}, u32[]{:S(2)}, u32[]{:S(2)}) async-start(bf16[1024,16,128]{2,0,1:T(8,128)(2,1)} %tile.5), calls=%async_computation.1 | async-start | bytes 8388608 | tf_op jit(solution)/shard_map/all_to_all | solution.py:99
  84.3 2.8 convert_reduce_fusion
  87.1 3.2 fusion.5
  90.4 0.8 slice_convert_fusion.1
  91.2 10.0 %multiply_convert_fusion = (bf16[1024,512]{1,0:T(8,128)(2,1)S(1)}, f32[1024,512]{1,0:T(8,128)}, f32[1024,512]{1,0:T(8,128)}) fusion(bf16[1024,512]{1,0:T(8,128)(2,1)S(1)} %copy-done.5, bf16[1024,512]{1,0:T(8,128)(2,1)S(1)} %get-tuple-element.42, f32[2048]{0:T(1024)S(1)} %bitcast.98, f32[2048]{0:T(1024)S(1)} %bitcast.95, f32[1024]{0:T(1024)S(1)} %add_rsqrt_fusion, ...), kind=kOutput, calls=%fused_computation.37 | convolution fusion | flops 2198339584 | bytes 11558912 | tf_op jit(solution)/shard_map/dot_general | solution.py:94
  101.2 1.0 copy-done.14
  102.2 4.4 %convolution_convert_fusion.1 = bf16[2048,1024]{1,0:T(8,128)(2,1)} fusion(bf16[1024,512]{1,0:T(8,128)(2,1)S(1)} %get-tuple-element.36, bf16[512,1024]{1,0:T(8,128)(2,1)S(1)} %copy-done.7, bf16[512,1024]{1,0:T(8,128)(2,1)S(1)} %copy-done.6), kind=kOutput, calls=%fused_computation.19 | convolution fusion | flops 2153775104 | bytes 7340032 | tf_op jit(solution)/shard_map/dot_general | solution.py:96
  106.6 38.0 %all-to-all-done.1 = bf16[1024,16,128]{2,0,1:T(8,128)(2,1)} async-done(((bf16[1024,16,128]{2,0,1:T(8,128)(2,1)}), bf16[1024,16,128]{2,0,1:T(8,128)(2,1)}, u32[]{:S(2)}, u32[]{:S(2)}) %all-to-all-start.1) | async-done | bytes 4194336 | tf_op jit(solution)/shard_map/all_to_all | solution.py:99
  144.6 4.9 %all-to-all-start.2 = ((bf16[16,128,1024]{2,1,0:T(8,128)(2,1)}), bf16[16,128,1024]{2,1,0:T(8,128)(2,1)}, u32[]{:S(2)}, u32[]{:S(2)}) async-start(bf16[16,128,1024]{2,1,0:T(8,128)(2,1)} %bitcast.79), calls=%async_computation.2 | async-start | bytes 8388608 | tf_op jit(solution)/shard_map/all_to_all | solution.py:103
  149.5 6.4 %copy.26 = bf16[1024,16,128]{0,2,1:T(8,128)(2,1)} copy(bf16[1024,16,128]{2,0,1:T(8,128)(2,1)} %all-to-all-done.1) | data formatting | bytes 8388608 | tf_op jit(solution)/shard_map/all_to_all | solution.py:99
  155.9 6.7 %add_convert_fusion.1 = bf16[1024,512]{1,0:T(8,128)(2,1)S(1)} fusion(f32[1024,512]{1,0:T(8,128)} %get-tuple-element.37, f32[1024,512]{1,0:T(8,128)} %get-tuple-element.52, bf16[1024,2048]{0,1:T(8,128)(2,1)} %bitcast.77, bf16[1024]{0:T(1024)(128)(2,1)S(1)} %convert_element_type.143, bf16[512,1024]{1,0:T(8,128)(2,1)} %get-tuple-element.41, ...), kind=kOutput, calls=%fused_computation.34 | convolution fusion | flops 2161115136 | bytes 11536384 | tf_op jit(solution)/shard_map/dot_general | solution.py:25
  162.7 6.1 %fusion.2 = (f32[1024]{0:T(1024)S(1)}, f32[2048]{0:T(1024)S(1)}, f32[1024]{0:T(1024)S(1)}, f32[2048]{0:T(1024)S(1)}, bf16[1024,2048]{1,0:T(8,128)(2,1)S(1)}) fusion(f32[2048]{0:T(1024)S(1)} %bitcast.96, bf16[1024,512]{1,0:T(8,128)(2,1)S(1)} %add_convert_fusion.1, bf16[1024,512]{1,0:T(8,128)(2,1)S(1)} %copy-done.5, ...), kind=kOutput, calls=%fused_computation.8 | convolution fusion | flops 2176837632 | bytes 11575296 | tf_op jit(solution)/shard_map/dot_general | solution.py:25
  168.8 3.1 copy_bitcast_fusion
  171.9 34.9 %all-to-all-done.2 = bf16[16,128,1024]{2,1,0:T(8,128)(2,1)} async-done(((bf16[16,128,1024]{2,1,0:T(8,128)(2,1)}), bf16[16,128,1024]{2,1,0:T(8,128)(2,1)}, u32[]{:S(2)}, u32[]{:S(2)}) %all-to-all-start.2) | async-done | bytes 4194336 | tf_op jit(solution)/shard_map/all_to_all | solution.py:103
  206.8 4.6 %all-to-all-start.7 = ((bf16[1024,16,128]{2,0,1:T(8,128)(2,1)}), bf16[1024,16,128]{2,0,1:T(8,128)(2,1)}, u32[]{:S(2)}, u32[]{:S(2)}) async-start(bf16[1024,16,128]{2,0,1:T(8,128)(2,1)} %copy_bitcast_fusion), calls=%async_computation.7 | async-start | bytes 8388608 | tf_op jit(solution)/shard_map/all_to_all | solution.py:114
  211.4 5.2 %convolution_convert_fusion.2 = bf16[2048,512]{1,0:T(8,128)(2,1)S(1)} fusion(bf16[1024,512]{1,0:T(8,128)(2,1)S(1)} %copy-done.17, f32[2048]{0:T(1024)S(1)} %bitcast.99, f32[2048]{0:T(1024)S(1)} %bitcast.97, f32[1024]{0:T(1024)S(1)} %add_rsqrt_fusion, f32[1024]{0:T(1024)S(1)} %broadcast_multiply_fusion, bf16[1032,16,128]{2,0,1:T(8,128)(2,1)} %all-to-all-done), kind=kOutput, calls=%fused_computation.25 | convolution fusion | flops 2161115136 | bytes 7364608 | tf_op jit(solution)/shard_map/dot_general | solution.py:19
  216.8 1.0 copy-done.15
  217.8 2.4 fusion.11
  220.2 1.3 copy-done.1
  221.5 1.1 constant_dynamic-slice_fusion.2
  222.6 2.6 convert_add_fusion.1
  225.3 0.4 collective-permute-done.3
  225.6 2.6 convert_add_fusion
  228.2 3.1 convert_reduce_fusion.3
  231.4 34.1 %all-to-all-done.7 = bf16[1024,16,128]{2,0,1:T(8,128)(2,1)} async-done(((bf16[1024,16,128]{2,0,1:T(8,128)(2,1)}), bf16[1024,16,128]{2,0,1:T(8,128)(2,1)}, u32[]{:S(2)}, u32[]{:S(2)}) %all-to-all-start.7) | async-done | bytes 4194336 | tf_op jit(solution)/shard_map/all_to_all | solution.py:114
  265.5 4.4 %all-to-all-start.3 = ((bf16[4,256,512]{2,1,0:T(8,128)(2,1)}), bf16[4,256,512]{2,1,0:T(8,128)(2,1)S(1)}, u32[]{:S(2)}, u32[]{:S(2)}) async-start(bf16[4,256,512]{2,1,0:T(8,128)(2,1)} %bitcast.7), calls=%async_computation.3 | async-start | bytes 2097152 | tf_op jit(solution)/shard_map/all_to_all | solution.py:49
  270.1 3.8 %collective-permute-done.4 = f32[2,3072]{1,0:T(2,128)S(1)} collective-permute-done((f32[2,3072]{1,0:T(2,128)S(1)}, f32[2,3072]{1,0:T(2,128)S(1)}, u32[]{:S(2)}, u32[]{:S(2)}) %collective-permute-start.4) | collective-permute-done | bytes 24608 | tf_op jit(solution)/shard_map/ppermute | solution.py:61
  274.0 6.8 %all-to-all-done.3 = bf16[4,256,512]{2,1,0:T(8,128)(2,1)S(1)} async-done(((bf16[4,256,512]{2,1,0:T(8,128)(2,1)}), bf16[4,256,512]{2,1,0:T(8,128)(2,1)S(1)}, u32[]{:S(2)}, u32[]{:S(2)}) %all-to-all-start.3) | async-done | bytes 1048608 | tf_op jit(solution)/shard_map/all_to_all | solution.py:49
  280.8 3.5 %all-to-all-start.5 = ((bf16[4,128,1024]{2,1,0:T(8,128)(2,1)}), bf16[4,128,1024]{2,1,0:T(8,128)(2,1)S(1)}, u32[]{:S(2)}, u32[]{:S(2)}) async-start(bf16[4,128,1024]{2,1,0:T(8,128)(2,1)} %bitcast.9), calls=%async_computation.5 | async-start | bytes 2097152 | tf_op jit(solution)/shard_map/all_to_all | solution.py:49
  284.4 1.5 collective-permute-start.6
  285.9 2.5 collective-permute-done.6
  288.3 2.4 collective-permute-start.7
  290.7 3.0 collective-permute-done.7
  294.1 0.9 collective-permute-done.8
  295.0 2.1 collective-permute-start.9
  297.1 0.2 reduce_sum.99
  297.4 1.1 broadcast_in_dim.13
  298.4 3.9 %all-to-all-start.4 = ((bf16[4,256,512]{2,1,0:T(8,128)(2,1)}), bf16[4,256,512]{2,1,0:T(8,128)(2,1)S(1)}, u32[]{:S(2)}, u32[]{:S(2)}) async-start(bf16[4,256,512]{2,1,0:T(8,128)(2,1)} %broadcast_in_dim.13), calls=%async_computation.4 | async-start | bytes 2097152 | tf_op jit(solution)/shard_map/all_to_all | solution.py:53
  302.4 5.4 %fusion.6 = f32[1024,2048]{1,0:T(8,128)} fusion(f32[1024]{0:T(1024)S(1)} %add_rsqrt_fusion, f32[1024]{0:T(1024)S(1)} %broadcast_multiply_fusion, bf16[1032,16,128]{2,0,1:T(8,128)(2,1)} %all-to-all-done), kind=kLoop, calls=%fused_computation.13 | loop fusion | flops 6291456 | bytes 12591104 | tf_op jit(solution)/shard_map/mul | solution.py:91
  307.8 3.6 %collective-permute-start.10 = (f32[2,2048]{1,0:T(2,128)S(1)}, f32[2,2048]{1,0:T(2,128)S(1)}, u32[]{:S(2)}, u32[]{:S(2)}) collective-permute-start(f32[2,2048]{1,0:T(2,128)S(1)} %add.81), channel_id=1, source_target_pairs={{0,64},{32,96},{64,0},{96,32},{1,65},{33,97},{65,1},{97,33},{2,66}... | collective-permute-start | bytes 49160 | tf_op jit(solution)/shard_map/ppermute | solution.py:61
  311.4 6.4 %collective-permute-done.10 = f32[2,2048]{1,0:T(2,128)S(1)} collective-permute-done((f32[2,2048]{1,0:T(2,128)S(1)}, f32[2,2048]{1,0:T(2,128)S(1)}, u32[]{:S(2)}, u32[]{:S(2)}) %collective-permute-start.10) | collective-permute-done | bytes 16416 | tf_op jit(solution)/shard_map/ppermute | solution.py:61
  317.9 0.5 fusion.25
  318.4 0.2 reduce_sum.100
  318.6 1.1 broadcast_in_dim.14
  319.7 3.5 %all-to-all-start.6 = ((bf16[4,128,1024]{2,1,0:T(8,128)(2,1)}), bf16[4,128,1024]{2,1,0:T(8,128)(2,1)S(1)}, u32[]{:S(2)}, u32[]{:S(2)}) async-start(bf16[4,128,1024]{2,1,0:T(8,128)(2,1)} %broadcast_in_dim.14), calls=%async_computation.6 | async-start | bytes 2097152 | tf_op jit(solution)/shard_map/all_to_all | solution.py:53
  323.3 0.8 copy.29
  324.2 2.8 convert_reduce_fusion.2
  327.0 0.3 mul.187
  327.3 1.8 bitcast_multiply_fusion.1
  329.1 8.4 %all-to-all-done.6 = bf16[4,128,1024]{2,1,0:T(8,128)(2,1)S(1)} async-done(((bf16[4,128,1024]{2,1,0:T(8,128)(2,1)}), bf16[4,128,1024]{2,1,0:T(8,128)(2,1)S(1)}, u32[]{:S(2)}, u32[]{:S(2)}) %all-to-all-start.6) | async-done | bytes 1048608 | tf_op jit(solution)/shard_map/all_to_all | solution.py:53
  337.5 0.2 mul.190
  337.7 2.1 bitcast_multiply_fusion
  339.7 2.4 add_convert_fusion.4
  (70 shorter events, 1.6 us)
Async XLA Ops:
  4.9 8.3 %copy-start.11 = (s32[8,4]{0,1:T(4,128)S(1)}, s32[8,4]{0,1:T(4,128)}, u32[]{:S(2)}) copy-start(s32[8,4]{0,1:T(4,128)} %param.16) | copy-start | bytes 388
  4.9 8.8 %copy-start.3 = (bf16[1024,512]{1,0:T(8,128)(2,1)S(1)}, bf16[1024,512]{1,0:T(8,128)(2,1)}, u32[]{:S(2)}) copy-start(bf16[1024,512]{1,0:T(8,128)(2,1)} %param.14) | copy-start | bytes 3145732
  4.9 72.0 %all-to-all-start = ((bf16[1032,16,128]{2,0,1:T(8,128)(2,1)}), bf16[1032,16,128]{2,0,1:T(8,128)(2,1)}, u32[]{:S(2)}, u32[]{:S(2)}) async-start(bf16[1032,16,128]{2,0,1:T(8,128)(2,1)} %tile.4), calls=%async_computation | async-start | bytes 8454144 | tf_op jit(solution)/shard_map/all_to_all | solution.py:75
  13.3 0.7 copy-start.12
  13.6 1.2 copy-start.4
  13.8 2.9 collective-permute-start
  15.0 4.0 %collective-permute-start.1 = (bf16[512,1024]{1,0:T(8,128)(2,1)S(1)}, bf16[512,1024]{1,0:T(8,128)(2,1)}, u32[]{:S(2)}, u32[]{:S(2)}) collective-permute-start(bf16[512,1024]{1,0:T(8,128)(2,1)S(1)} %bitcast_multiply_fusion.2), channel_id=1, source_target_pairs={{0,16},{16,0},{1,17},{17,1},{2,18},{18,2},{3,19},{19,3},{4,20},{20... | collective-permute-start | bytes 3145736 | tf_op jit(solution)/shard_map/ppermute | solution.py:31
  19.0 57.8 %copy-start.9 = (bf16[1024,128]{1,0:T(8,128)(2,1)S(1)}, bf16[1024,128]{1,0:T(8,128)(2,1)}, u32[]{:S(2)}) copy-start(bf16[1024,128]{1,0:T(8,128)(2,1)} %param.10) | copy-start | bytes 786436
  79.6 65.0 %all-to-all-start.1 = ((bf16[1024,16,128]{2,0,1:T(8,128)(2,1)}), bf16[1024,16,128]{2,0,1:T(8,128)(2,1)}, u32[]{:S(2)}, u32[]{:S(2)}) async-start(bf16[1024,16,128]{2,0,1:T(8,128)(2,1)} %tile.5), calls=%async_computation.1 | async-start | bytes 8388608 | tf_op jit(solution)/shard_map/all_to_all | solution.py:99
  87.1 4.1 %copy-start.5 = (bf16[1024,512]{1,0:T(8,128)(2,1)S(1)}, bf16[1024,512]{1,0:T(8,128)(2,1)}, u32[]{:S(2)}) copy-start(bf16[1024,512]{1,0:T(8,128)(2,1)} %get-tuple-element.43) | copy-start | bytes 3145732
  91.2 11.0 %copy-start.6 = (bf16[512,1024]{1,0:T(8,128)(2,1)S(1)}, bf16[512,1024]{1,0:T(8,128)(2,1)}, u32[]{:S(2)}) copy-start(bf16[512,1024]{1,0:T(8,128)(2,1)} %get-tuple-element.40) | copy-start | bytes 3145732
  91.2 11.0 %copy-start.7 = (bf16[512,1024]{1,0:T(8,128)(2,1)S(1)}, bf16[512,1024]{1,0:T(8,128)(2,1)}, u32[]{:S(2)}) copy-start(bf16[512,1024]{1,0:T(8,128)(2,1)} %get-tuple-element.41) | copy-start | bytes 3145732
  101.2 1.0 copy-start.14
  144.6 4.9 %copy-start.10 = (s32[1024]{0:T(1024)S(1)}, s32[1024]{0:T(1024)}, u32[]{:S(2)}) copy-start(s32[1024]{0:T(1024)} %param.11) | copy-start | bytes 12292
  144.6 62.2 %all-to-all-start.2 = ((bf16[16,128,1024]{2,1,0:T(8,128)(2,1)}), bf16[16,128,1024]{2,1,0:T(8,128)(2,1)}, u32[]{:S(2)}, u32[]{:S(2)}) async-start(bf16[16,128,1024]{2,1,0:T(8,128)(2,1)} %bitcast.79), calls=%async_computation.2 | async-start | bytes 8388608 | tf_op jit(solution)/shard_map/all_to_all | solution.py:103
  162.7 6.1 %copy-start.16 = (bf16[1024,512]{1,0:T(8,128)(2,1)}, bf16[1024,512]{1,0:T(8,128)(2,1)S(1)}, u32[]{:S(2)}) copy-start(bf16[1024,512]{1,0:T(8,128)(2,1)S(1)} %add_convert_fusion.1) | copy-start | bytes 3145732
  171.9 39.5 %copy-start.17 = (bf16[1024,512]{1,0:T(8,128)(2,1)S(1)}, bf16[1024,512]{1,0:T(8,128)(2,1)}, u32[]{:S(2)}) copy-start(bf16[1024,512]{1,0:T(8,128)(2,1)} %copy-done.16) | copy-start | bytes 3145732
  206.8 58.7 %all-to-all-start.7 = ((bf16[1024,16,128]{2,0,1:T(8,128)(2,1)}), bf16[1024,16,128]{2,0,1:T(8,128)(2,1)}, u32[]{:S(2)}, u32[]{:S(2)}) async-start(bf16[1024,16,128]{2,0,1:T(8,128)(2,1)} %copy_bitcast_fusion), calls=%async_computation.7 | async-start | bytes 8388608 | tf_op jit(solution)/shard_map/all_to_all | solution.py:114
  211.4 5.4 %copy-start = (bf16[1024,16,128]{0,2,1:T(8,128)(2,1)S(1)}, bf16[1024,16,128]{0,2,1:T(8,128)(2,1)}, u32[]{:S(2)}) copy-start(bf16[1024,16,128]{0,2,1:T(8,128)(2,1)} %copy.26) | copy-start | bytes 12582916
  216.6 1.2 copy-start.15
  216.7 5.9 %collective-permute-start.2 = (bf16[1024,512]{1,0:T(8,128)(2,1)S(1)}, bf16[1024,512]{1,0:T(8,128)(2,1)}, u32[]{:S(2)}, u32[]{:S(2)}) collective-permute-start(bf16[1024,512]{1,0:T(8,128)(2,1)S(1)} %constant_dynamic-slice_fusion.3), channel_id=1, source_target_pairs={{0,16},{16,0},{1,17},{17,1},{2,18},{18,2},{3,19},{19,3},{4,20},{20... | collective-permute-start | bytes 3145736 | tf_op jit(solution)/shard_map/ppermute | solution.py:43
  220.2 1.3 copy-start.1
  222.6 3.0 collective-permute-start.3
  222.6 3.0 copy-start.2
  265.5 28.4 %copy-start.8 = (bf16[1024,128]{1,0:T(8,128)(2,1)S(1)}, bf16[1024,128]{1,0:T(8,128)(2,1)}, u32[]{:S(2)}) copy-start(bf16[1024,128]{1,0:T(8,128)(2,1)} %param.9) | copy-start | bytes 786436
  265.5 28.5 %copy-start.13 = (bf16[128]{0:T(256)(128)(2,1)S(1)}, bf16[128]{0:T(256)(128)(2,1)}, u32[]{:S(2)}) copy-start(bf16[128]{0:T(256)(128)(2,1)} %param.12) | copy-start | bytes 772
  265.5 15.3 %all-to-all-start.3 = ((bf16[4,256,512]{2,1,0:T(8,128)(2,1)}), bf16[4,256,512]{2,1,0:T(8,128)(2,1)S(1)}, u32[]{:S(2)}, u32[]{:S(2)}) async-start(bf16[4,256,512]{2,1,0:T(8,128)(2,1)} %bitcast.7), calls=%async_computation.3 | async-start | bytes 2097152 | tf_op jit(solution)/shard_map/all_to_all | solution.py:49
  270.0 3.9 %collective-permute-start.4 = (f32[2,3072]{1,0:T(2,128)S(1)}, f32[2,3072]{1,0:T(2,128)S(1)}, u32[]{:S(2)}, u32[]{:S(2)}) collective-permute-start(f32[2,3072]{1,0:T(2,128)S(1)} %maximum_maximum_fusion), channel_id=1, source_target_pairs={{0,1},{1,0},{2,3},{3,2},{4,5},{5,4},{6,7},{7,6},{8,9},{9,8},{10,11... | collective-permute-start | bytes 73736 | tf_op jit(solution)/shard_map/ppermute | solution.py:61
  273.9 10.5 %collective-permute-start.5 = (f32[2,3072]{1,0:T(2,128)S(1)}, f32[2,3072]{1,0:T(2,128)S(1)}, u32[]{:S(2)}, u32[]{:S(2)}) collective-permute-start(f32[2,3072]{1,0:T(2,128)S(1)} %fusion.39), channel_id=1, source_target_pairs={{0,2},{1,3},{2,0},{3,1},{4,6},{5,7},{6,4},{7,5},{8,10},{9,11},{10,... | collective-permute-start | bytes 73736 | tf_op jit(solution)/shard_map/ppermute | solution.py:61
  280.8 16.5 %all-to-all-start.5 = ((bf16[4,128,1024]{2,1,0:T(8,128)(2,1)}), bf16[4,128,1024]{2,1,0:T(8,128)(2,1)S(1)}, u32[]{:S(2)}, u32[]{:S(2)}) async-start(bf16[4,128,1024]{2,1,0:T(8,128)(2,1)} %bitcast.9), calls=%async_computation.5 | async-start | bytes 2097152 | tf_op jit(solution)/shard_map/all_to_all | solution.py:49
  284.4 3.9 %collective-permute-start.6 = (f32[2,3072]{1,0:T(2,128)S(1)}, f32[2,3072]{1,0:T(2,128)S(1)}, u32[]{:S(2)}, u32[]{:S(2)}) collective-permute-start(f32[2,3072]{1,0:T(2,128)S(1)} %fusion.40), channel_id=1, source_target_pairs={{0,4},{1,5},{2,6},{3,7},{4,0},{5,1},{6,2},{7,3},{8,12},{9,13},{10,... | collective-permute-start | bytes 73736 | tf_op jit(solution)/shard_map/ppermute | solution.py:61
  288.3 5.4 %collective-permute-start.7 = (f32[2,3072]{1,0:T(2,128)S(1)}, f32[2,3072]{1,0:T(2,128)S(1)}, u32[]{:S(2)}, u32[]{:S(2)}) collective-permute-start(f32[2,3072]{1,0:T(2,128)S(1)} %add.76), channel_id=1, source_target_pairs={{0,8},{1,9},{2,10},{3,11},{4,12},{5,13},{6,14},{7,15},{8,0},{9,1},... | collective-permute-start | bytes 73736 | tf_op jit(solution)/shard_map/ppermute | solution.py:61
  293.8 1.3 collective-permute-start.8
  295.0 12.7 %collective-permute-start.9 = (f32[2,2048]{1,0:T(2,128)S(1)}, f32[2,2048]{1,0:T(2,128)S(1)}, u32[]{:S(2)}, u32[]{:S(2)}) collective-permute-start(f32[2,2048]{1,0:T(2,128)S(1)} %slice_add_fusion), channel_id=1, source_target_pairs={{0,32},{32,0},{64,96},{96,64},{1,33},{33,1},{65,97},{97,65},{2,34}... | collective-permute-start | bytes 49160 | tf_op jit(solution)/shard_map/ppermute | solution.py:61
  298.4 20.2 %all-to-all-start.4 = ((bf16[4,256,512]{2,1,0:T(8,128)(2,1)}), bf16[4,256,512]{2,1,0:T(8,128)(2,1)S(1)}, u32[]{:S(2)}, u32[]{:S(2)}) async-start(bf16[4,256,512]{2,1,0:T(8,128)(2,1)} %broadcast_in_dim.13), calls=%async_computation.4 | async-start | bytes 2097152 | tf_op jit(solution)/shard_map/all_to_all | solution.py:53
  307.8 10.1 %collective-permute-start.10 = (f32[2,2048]{1,0:T(2,128)S(1)}, f32[2,2048]{1,0:T(2,128)S(1)}, u32[]{:S(2)}, u32[]{:S(2)}) collective-permute-start(f32[2,2048]{1,0:T(2,128)S(1)} %add.81), channel_id=1, source_target_pairs={{0,64},{32,96},{64,0},{96,32},{1,65},{33,97},{65,1},{97,33},{2,66}... | collective-permute-start | bytes 49160 | tf_op jit(solution)/shard_map/ppermute | solution.py:61
  319.7 17.7 %all-to-all-start.6 = ((bf16[4,128,1024]{2,1,0:T(8,128)(2,1)}), bf16[4,128,1024]{2,1,0:T(8,128)(2,1)S(1)}, u32[]{:S(2)}, u32[]{:S(2)}) async-start(bf16[4,128,1024]{2,1,0:T(8,128)(2,1)} %broadcast_in_dim.14), calls=%async_computation.6 | async-start | bytes 2097152 | tf_op jit(solution)/shard_map/all_to_all | solution.py:53

commit v3 on v0

--- a/solution.py
+++ b/solution.py
@@ -71,11 +71,13 @@
     stacked = jnp.concatenate(
         [tokens, ln_gain[None], ln_bias[None], jnp.zeros((6, tokens.shape[1]), tokens.dtype)]
     )
-    gathered = lax.all_to_all(
-        jnp.tile(stacked, (1, sizes["tp"])), "tp", split_axis=1, concat_axis=1, tiled=True
-    )
+    gathered = lax.all_gather(stacked, "tp", axis=1, tiled=True)
     whole_rows = gathered[:frames]
     gain_full, bias_full = gathered[frames], gathered[frames + 1]
+    cot_copies, whole_rows = lax.optimization_barrier(
+        (jnp.tile(cotangent, (1, sizes["tp"])), whole_rows)
+    )
+    whole_grad = lax.all_to_all(cot_copies, "tp", split_axis=1, concat_axis=1, tiled=True)
     masked_in = apply_blocks(weight_in, blocks_in, jnp.bfloat16)
     masked_out = apply_blocks(weight_out, blocks_out, jnp.bfloat16)
     full_in = pair_gather(masked_in, 0)
@@ -96,7 +98,6 @@
     partial_out = lax.dot_general(
         full_out, active, (((0,), (1,)), ((), ())), preferred_element_type=jnp.float32
     ).astype(jnp.bfloat16)
-    whole_grad = lax.all_gather(cotangent, "tp", axis=1, tiled=True)
     unused, whole_grad = lax.optimization_barrier((partial_out, whole_grad))
     branch = lax.psum_scatter(
         partial_out, "tp", scatter_dimension=0, tiled=True

time: 286 us -> 315 us (1.10)
  blocking collectives: 0 us -> 19.4 us
  waiting for transfers between devices: 139 us -> 158 us
  local copies, waits for them, and re-layouts: 23.6 us -> 40.6 us
  starting transfers between devices: 38.8 us -> 24.7 us
  other arithmetic: 31 us -> 21.3 us
  matrix products: 38.1 us -> 34.9 us
    all_gather x1, waiting for transfers between devices: 3.7 us -> 51.5 us  [on_device(): gathered = lax.all_gather(stacked, 'tp', axis=1, tiled=True)]
    reduce_scatter x1, waiting for transfers between devices: 40.1 us -> 0.01 us  [on_device(): lax.psum_scatter(partial_out, 'tp', scatter_dimension=0, tiled=True)]
    all_to_all x0 -> x1, blocking collectives: none -> 19.4 us  [rows_allreduce(): lax.all_to_all(term.astype(jnp.bfloat16), axis, split_axis=0, concat_axis...]
    all_to_all x0 -> x2, local copies, waits for them, and re-layouts: none -> 12.9 us  [on_device(): lax.all_to_all(cot_copies, 'tp', split_axis=1, concat_axis=1, tiled=True)]
    all_to_all x1, waiting for transfers between devices: 57.2 us -> 69 us  [on_device(): lax.all_to_all(cot_copies, 'tp', split_axis=1, concat_axis=1, tiled=True)]
    ppermute x7, starting transfers between devices: 14.4 us -> 7.21 us  [butterfly_sum(): values = values + lax.ppermute(values, axis, perm=perm)]
    mul x1, other arithmetic: 5.48 us -> 0.85 us  [on_device(): normed * gain_f + bias_full.astype(jnp.float32)]
    all_to_all x2 -> x1, starting transfers between devices: 7.86 us -> 3.52 us  [rows_allreduce(): lax.all_to_all(term.astype(jnp.bfloat16), axis, split_axis=0, concat_axis...]
  transfers between devices with their start and end apart: 19 -> 18, of which waited for: 13 -> 12; matrix products, arithmetic and copies ran while one was open for 28% -> 20% of each run, Pallas kernels for 0% -> 0%
where the time goes in v3:
time: 315 us; the launch traced here: 314 us
  waiting for transfers between devices  158 us (50%)
  local copies, waits for them, and re-layouts  40.6 us (13%)
  matrix products  34.9 us (11%)
  starting transfers between devices  24.7 us (8%)
  other arithmetic  21.3 us (7%)
  blocking collectives  19.4 us (6%)
  between operations  14.3 us (5%)
    all_to_all x1, waiting for transfers between devices, on_device(): lax.all_to_all(cot_copies, 'tp', split_axis=1, concat_axis=1, tiled=True)  69 us
    all_gather x1, waiting for transfers between devices, on_device(): gathered = lax.all_gather(stacked, 'tp', axis=1, tiled=True)  51.5 us
    all_to_all x1, blocking collectives, rows_allreduce(): lax.all_to_all(term.astype(jnp.bfloat16), axis, split_axis=0, concat_axis...  19.4 us
    ppermute x7, waiting for transfers between devices, butterfly_sum(): values = values + lax.ppermute(values, axis, perm=perm)  16.7 us
    unnamed x47, local copies, waits for them, and re-layouts  15.4 us
    dot_general x2, matrix products, contract_cols(): lax.dot_general(left, right, (((1,), (1,)), ((), ())), preferred_element_...  14.1 us
    all_to_all x2, local copies, waits for them, and re-layouts, on_device(): lax.all_to_all(cot_copies, 'tp', split_axis=1, concat_axis=1, tiled=True)  12.9 us
    all_to_all x2, waiting for transfers between devices, rows_allreduce(): lax.all_to_all(copies, axis, split_axis=0, concat_axis=0, tiled=True)  9.59 us
  transfers between devices with their start and end apart: 18, of which 12 were waited for; matrix products, arithmetic and copies ran while one was open for 20% of the time, Pallas kernels for 0%

profile of v3, /device:TPU:0, one launch (start us, length us, event | category | flops | bytes accessed | tf_op | source)
XLA Modules:
  0.0 313.7 jit_solution(12835107658097667314)
XLA Ops:
  7.2 3.0 concatenate.12
  10.3 0.8 fusion.36
  11.1 0.3 mul.170
  11.5 0.2 bitcast_multiply_fusion.3
  11.8 0.2 mul.174
  12.0 0.7 copy-done.7
  13.0 0.1 copy.24
  13.1 1.4 collective-permute-done
  14.6 2.3 broadcast_select_fusion.3
  16.9 2.7 broadcast_select_fusion.1
  19.6 51.5 %all-gather.2.cloned.1.call-done = bf16[1032,2048]{1,0:T(8,128)(2,1)} async-done(((bf16[1032,128]{1,0:T(8,128)(2,1)}), bf16[1032,2048]{1,0:T(8,128)(2,1)}) %all-gather.2.cloned.1.call-update) | async-done | bytes 4227088 | tf_op jit(solution)/shard_map/all_gather | solution.py:74
  71.1 2.5 slice.35
  73.6 2.8 tile.4
  76.4 0.6 convert_reduce_fusion.1
  77.0 1.2 fusion.5
  78.3 0.9 slice_convert_fusion.1
  79.2 8.6 %multiply_convert_fusion = (bf16[1024,512]{1,0:T(8,128)(2,1)S(1)}, f32[1024,512]{1,0:T(8,128)}, f32[1024,512]{1,0:T(8,128)}) fusion(bf16[1024,512]{1,0:T(8,128)(2,1)S(1)} %copy-done.8, bf16[1024,512]{1,0:T(8,128)(2,1)S(1)} %get-tuple-element.53, f32[2048]{0:T(1024)S(1)} %bitcast.75, f32[2048]{0:T(1024)S(1)} %bitcast.72, f32[1024]{0:T(1024)S(1)} %add_rsqrt_fusion, ...), kind=kOutput, calls=%fused_computation.32 | convolution fusion | flops 2198339584 | bytes 11558912 | tf_op jit(solution)/shard_map/dot_general | solution.py:96
  87.7 1.0 copy-done.17
  88.8 4.6 %convolution_convert_fusion.1 = bf16[2048,1024]{1,0:T(8,128)(2,1)} fusion(bf16[1024,512]{1,0:T(8,128)(2,1)S(1)} %get-tuple-element.46, bf16[512,1024]{1,0:T(8,128)(2,1)S(1)} %copy-done.10, bf16[512,1024]{1,0:T(8,128)(2,1)S(1)} %copy-done.9), kind=kOutput, calls=%fused_computation.14 | convolution fusion | flops 2153775104 | bytes 7340032 | tf_op jit(solution)/shard_map/dot_general | solution.py:98
  93.4 6.4 %copy.26 = bf16[1024,16,128]{2,0,1:T(8,128)(2,1)} copy(bf16[1024,16,128]{0,2,1:T(8,128)(2,1)} %tile.4) | data formatting | bytes 8388608 | tf_op jit(solution)/shard_map/all_to_all | solution.py:80
  99.8 5.1 %all-to-all-start = ((bf16[1024,16,128]{2,0,1:T(8,128)(2,1)}), bf16[1024,16,128]{2,0,1:T(8,128)(2,1)}, u32[]{:S(2)}, u32[]{:S(2)}) async-start(bf16[1024,16,128]{2,0,1:T(8,128)(2,1)} %copy.26), calls=%async_computation | async-start | bytes 8388608 | tf_op jit(solution)/shard_map/all_to_all | solution.py:80
  105.0 69.0 %all-to-all-done = bf16[1024,16,128]{2,0,1:T(8,128)(2,1)} async-done(((bf16[1024,16,128]{2,0,1:T(8,128)(2,1)}), bf16[1024,16,128]{2,0,1:T(8,128)(2,1)}, u32[]{:S(2)}, u32[]{:S(2)}) %all-to-all-start) | async-done | bytes 4194336 | tf_op jit(solution)/shard_map/all_to_all | solution.py:80
  174.0 6.5 %copy.27 = bf16[1024,16,128]{0,2,1:T(8,128)(2,1)} copy(bf16[1024,16,128]{2,0,1:T(8,128)(2,1)} %all-to-all-done) | data formatting | bytes 8388608 | tf_op jit(solution)/shard_map/all_to_all | solution.py:80
  180.5 7.1 %add_convert_fusion.1 = bf16[1024,512]{1,0:T(8,128)(2,1)S(1)} fusion(f32[1024,512]{1,0:T(8,128)} %get-tuple-element.47, f32[1024,512]{1,0:T(8,128)} %get-tuple-element.63, bf16[1024,2048]{0,1:T(8,128)(2,1)} %bitcast.54, bf16[1024]{0:T(1024)(128)(2,1)S(1)} %convert_element_type.111, bf16[512,1024]{1,0:T(8,128)(2,1)} %get-tuple-element.52, ...), kind=kOutput, calls=%fused_computation.29 | convolution fusion | flops 2161115136 | bytes 11536384 | tf_op jit(solution)/shard_map/dot_general | solution.py:25
  187.6 7.0 %fusion.4 = (f32[1024]{0:T(1024)S(1)}, f32[2048]{0:T(1024)S(1)}, f32[1024]{0:T(1024)S(1)}, f32[2048]{0:T(1024)S(1)}, f32[1024,2048]{1,0:T(8,128)}, /*index=5*/bf16[1024,2048]{1,0:T(8,128)(2,1)}) fusion(f32[2048]{0:T(1024)S(1)} %bitcast.73, f32[1024]{0:T(1024)S(1)} %add_rsqrt_fusion, f32[1024]{0:T(1024)S(1)} %broadcast_multiply_fusion, ...), kind=kOutput, calls=%fused_computation.9 | convolution fusion | flops 2176837632 | bytes 19963904 | tf_op jit(solution)/shard_map/dot_general | solution.py:25
  194.6 6.4 %copy.30 = bf16[1024,2048]{0,1:T(8,128)(2,1)} copy(bf16[1024,2048]{1,0:T(8,128)(2,1)} %get-tuple-element.64) | data formatting | bytes 8388608
  201.0 1.2 copy-done.20
  202.2 5.2 %convolution_convert_fusion.2 = bf16[2048,512]{1,0:T(8,128)(2,1)S(1)} fusion(bf16[1024,512]{1,0:T(8,128)(2,1)S(1)} %copy-done.20, f32[2048]{0:T(1024)S(1)} %bitcast.76, f32[2048]{0:T(1024)S(1)} %bitcast.74, bf16[1024,2048]{1,0:T(8,128)(2,1)} %copy-done, f32[1024]{0:T(1024)S(1)} %add_rsqrt_fusion, f32[1024]{0:T(1024)S(1)} %broadcast_multiply_fusion), kind=kOutput, calls=%fused_computation.20 | convolution fusion | flops 2161115136 | bytes 7364608 | tf_op jit(solution)/shard_map/dot_general | solution.py:19
  207.5 1.3 copy-done.3
  209.0 1.0 copy-done.18
  210.0 2.4 fusion.11
  212.5 1.3 copy-done.4
  213.9 0.3 collective-permute-start.3
  214.2 2.0 convert_add_fusion.1
  216.2 0.8 collective-permute-done.3
  217.0 2.6 convert_add_fusion
  219.6 1.0 convert_bitcast_fusion
  220.6 19.4 %all_to_all.42 = bf16[4,256,512]{2,1,0:T(8,128)(2,1)S(1)} all-to-all(bf16[4,256,512]{2,1,0:T(8,128)(2,1)S(1)} %bitcast.56), channel_id=1, replica_groups=mesh['rep'=4,'fsdp'=2,'tp'=16] {'rep'}, dimensions={0} | all-to-all | bytes 2097152 | tf_op jit(solution)/shard_map/all_to_all | solution.py:49
  240.0 3.5 %all-to-all-start.3 = ((bf16[4,128,1024]{2,1,0:T(8,128)(2,1)}), bf16[4,128,1024]{2,1,0:T(8,128)(2,1)S(1)}, u32[]{:S(2)}, u32[]{:S(2)}) async-start(bf16[4,128,1024]{2,1,0:T(8,128)(2,1)} %bitcast.10), calls=%async_computation.4 | async-start | bytes 2097152 | tf_op jit(solution)/shard_map/all_to_all | solution.py:49
  243.6 4.1 %collective-permute-done.4 = f32[2,3072]{1,0:T(2,128)S(1)} collective-permute-done((f32[2,3072]{1,0:T(2,128)S(1)}, f32[2,3072]{1,0:T(2,128)S(1)}, u32[]{:S(2)}, u32[]{:S(2)}) %collective-permute-start.4) | collective-permute-done | bytes 24608 | tf_op jit(solution)/shard_map/ppermute | solution.py:61
  247.9 0.2 reduce_sum.80
  248.1 9.6 %all-to-all-done.3 = bf16[4,128,1024]{2,1,0:T(8,128)(2,1)S(1)} async-done(((bf16[4,128,1024]{2,1,0:T(8,128)(2,1)}), bf16[4,128,1024]{2,1,0:T(8,128)(2,1)S(1)}, u32[]{:S(2)}, u32[]{:S(2)}) %all-to-all-start.3) | async-done | bytes 1048608 | tf_op jit(solution)/shard_map/all_to_all | solution.py:49
  257.7 1.1 broadcast_in_dim.13
  258.7 3.5 %all-to-all-start.2 = ((bf16[4,256,512]{2,1,0:T(8,128)(2,1)}), bf16[4,256,512]{2,1,0:T(8,128)(2,1)S(1)}, u32[]{:S(2)}, u32[]{:S(2)}) async-start(bf16[4,256,512]{2,1,0:T(8,128)(2,1)} %broadcast_in_dim.13), calls=%async_computation.3 | async-start | bytes 2097152 | tf_op jit(solution)/shard_map/all_to_all | solution.py:53
  262.4 4.0 %collective-permute-done.6 = f32[2,3072]{1,0:T(2,128)S(1)} collective-permute-done((f32[2,3072]{1,0:T(2,128)S(1)}, f32[2,3072]{1,0:T(2,128)S(1)}, u32[]{:S(2)}, u32[]{:S(2)}) %collective-permute-start.6) | collective-permute-done | bytes 24608 | tf_op jit(solution)/shard_map/ppermute | solution.py:61
  266.4 1.5 collective-permute-start.7
  267.9 3.9 %collective-permute-done.7 = f32[2,3072]{1,0:T(2,128)S(1)} collective-permute-done((f32[2,3072]{1,0:T(2,128)S(1)}, f32[2,3072]{1,0:T(2,128)S(1)}, u32[]{:S(2)}, u32[]{:S(2)}) %collective-permute-start.7) | collective-permute-done | bytes 24608 | tf_op jit(solution)/shard_map/ppermute | solution.py:61
  271.9 1.2 collective-permute-done.8
  273.1 1.9 collective-permute-start.9
  275.3 1.6 collective-permute-done.9
  276.9 3.4 %collective-permute-start.10 = (f32[2,2048]{1,0:T(2,128)S(1)}, f32[2,2048]{1,0:T(2,128)S(1)}, u32[]{:S(2)}, u32[]{:S(2)}) collective-permute-start(f32[2,2048]{1,0:T(2,128)S(1)} %add.92), channel_id=1, source_target_pairs={{0,64},{32,96},{64,0},{96,32},{1,65},{33,97},{65,1},{97,33},{2,66}... | collective-permute-start | bytes 49160 | tf_op jit(solution)/shard_map/ppermute | solution.py:61
  280.4 1.9 collective-permute-done.10
  282.3 0.2 reduce_sum.81
  282.5 1.1 broadcast_in_dim.14
  283.6 4.6 %all-to-all-start.4 = ((bf16[4,128,1024]{2,1,0:T(8,128)(2,1)}), bf16[4,128,1024]{2,1,0:T(8,128)(2,1)S(1)}, u32[]{:S(2)}, u32[]{:S(2)}) async-start(bf16[4,128,1024]{2,1,0:T(8,128)(2,1)} %broadcast_in_dim.14), calls=%async_computation.5 | async-start | bytes 2097152 | tf_op jit(solution)/shard_map/all_to_all | solution.py:53
  288.2 0.5 fusion.25
  288.8 0.8 copy.29
  289.6 0.3 mul.193
  290.0 1.8 bitcast_multiply_fusion.1
  291.7 9.6 %all-to-all-done.4 = bf16[4,128,1024]{2,1,0:T(8,128)(2,1)S(1)} async-done(((bf16[4,128,1024]{2,1,0:T(8,128)(2,1)}), bf16[4,128,1024]{2,1,0:T(8,128)(2,1)S(1)}, u32[]{:S(2)}, u32[]{:S(2)}) %all-to-all-start.4) | async-done | bytes 1048608 | tf_op jit(solution)/shard_map/all_to_all | solution.py:53
  301.3 0.2 mul.196
  301.5 2.1 bitcast_multiply_fusion
  303.6 1.1 copy.31
  304.8 2.4 add_convert_fusion.4
  (80 shorter events, 1.8 us)
Async XLA Ops:
  7.2 4.3 %copy-start.6 = (bf16[1024,512]{1,0:T(8,128)(2,1)S(1)}, bf16[1024,512]{1,0:T(8,128)(2,1)}, u32[]{:S(2)}) copy-start(bf16[1024,512]{1,0:T(8,128)(2,1)} %param.14) | copy-start | bytes 3145732
  7.2 63.9 %all-gather.2.cloned.1.call-start = ((), (), s32[]{:S(2)}) async-start(), calls=%async_computation.7 | async-start | bytes 4491264 | tf_op jit(solution)/shard_map/all_gather | solution.py:74
  10.2 209.3 %reduce-scatter.5.cloned.1.call-start = ((), (), s32[]{:S(2)}) async-start(), calls=%async_computation.8 | async-start | bytes 4456448 | tf_op jit(solution)/shard_map/reduce_scatter | solution.py:102
  11.1 0.7 copy-start.15
  11.5 1.2 copy-start.7
  11.7 2.9 collective-permute-start
  11.8 1.1 copy-start.12
  12.9 4.0 %collective-permute-start.1 = (bf16[512,1024]{1,0:T(8,128)(2,1)S(1)}, bf16[512,1024]{1,0:T(8,128)(2,1)}, u32[]{:S(2)}, u32[]{:S(2)}) collective-permute-start(bf16[512,1024]{1,0:T(8,128)(2,1)S(1)} %bitcast_multiply_fusion.2), channel_id=1, source_target_pairs={{0,16},{16,0},{1,17},{17,1},{2,18},{18,2},{3,19},{19,3},{4,20},{20... | collective-permute-start | bytes 3145736 | tf_op jit(solution)/shard_map/ppermute | solution.py:31
  73.6 5.5 %copy-start = (bf16[1024,2048]{1,0:T(8,128)(2,1)}, bf16[1024,2048]{1,0:T(8,128)(2,1)S(1)}, u32[]{:S(2)}) copy-start(bf16[1024,2048]{1,0:T(8,128)(2,1)S(1)} %slice.35) | copy-start | bytes 12582916
  77.0 2.1 copy-start.8
  79.1 9.6 %copy-start.9 = (bf16[512,1024]{1,0:T(8,128)(2,1)S(1)}, bf16[512,1024]{1,0:T(8,128)(2,1)}, u32[]{:S(2)}) copy-start(bf16[512,1024]{1,0:T(8,128)(2,1)} %get-tuple-element.51) | copy-start | bytes 3145732
  79.2 9.6 %copy-start.10 = (bf16[512,1024]{1,0:T(8,128)(2,1)S(1)}, bf16[512,1024]{1,0:T(8,128)(2,1)}, u32[]{:S(2)}) copy-start(bf16[512,1024]{1,0:T(8,128)(2,1)} %get-tuple-element.52) | copy-start | bytes 3145732
  87.7 1.0 copy-start.17
  99.8 5.2 %copy-start.14 = (s32[1024]{0:T(1024)S(1)}, s32[1024]{0:T(1024)}, u32[]{:S(2)}) copy-start(s32[1024]{0:T(1024)} %param.11) | copy-start | bytes 12292
  99.8 74.2 %all-to-all-start = ((bf16[1024,16,128]{2,0,1:T(8,128)(2,1)}), bf16[1024,16,128]{2,0,1:T(8,128)(2,1)}, u32[]{:S(2)}, u32[]{:S(2)}) async-start(bf16[1024,16,128]{2,0,1:T(8,128)(2,1)} %copy.26), calls=%async_computation | async-start | bytes 8388608 | tf_op jit(solution)/shard_map/all_to_all | solution.py:80
  104.9 198.7 %reduce-scatter.7.cloned.1.call-start = ((), (), s32[]{:S(2)}) async-start(), calls=%async_computation.9 | async-start | bytes 4456448
  180.5 7.1 %copy-start.1 = (bf16[1024,2048]{1,0:T(8,128)(2,1)S(1)}, bf16[1024,2048]{1,0:T(8,128)(2,1)}, u32[]{:S(2)}) copy-start(bf16[1024,2048]{1,0:T(8,128)(2,1)} %copy-done) | copy-start | bytes 12582916
  187.6 7.0 %copy-start.19 = (bf16[1024,512]{1,0:T(8,128)(2,1)}, bf16[1024,512]{1,0:T(8,128)(2,1)S(1)}, u32[]{:S(2)}) copy-start(bf16[1024,512]{1,0:T(8,128)(2,1)S(1)} %add_convert_fusion.1) | copy-start | bytes 3145732
  201.0 1.2 copy-start.20
  202.2 6.7 %copy-start.2 = (bf16[1024,16,128]{0,2,1:T(8,128)(2,1)S(1)}, bf16[1024,16,128]{0,2,1:T(8,128)(2,1)}, u32[]{:S(2)}) copy-start(bf16[1024,16,128]{0,2,1:T(8,128)(2,1)} %copy.27) | copy-start | bytes 12582916
  207.5 1.3 copy-start.3
  208.8 1.2 copy-start.18
  208.9 5.3 %collective-permute-start.2 = (bf16[1024,512]{1,0:T(8,128)(2,1)S(1)}, bf16[1024,512]{1,0:T(8,128)(2,1)}, u32[]{:S(2)}, u32[]{:S(2)}) collective-permute-start(bf16[1024,512]{1,0:T(8,128)(2,1)S(1)} %constant_dynamic-slice_fusion.3), channel_id=1, source_target_pairs={{0,16},{16,0},{1,17},{17,1},{2,18},{18,2},{3,19},{19,3},{4,20},{20... | collective-permute-start | bytes 3145736 | tf_op jit(solution)/shard_map/ppermute | solution.py:43
  212.4 1.3 copy-start.4
  213.9 3.1 collective-permute-start.3
  214.2 2.8 copy-start.5
  240.0 17.7 %all-to-all-start.3 = ((bf16[4,128,1024]{2,1,0:T(8,128)(2,1)}), bf16[4,128,1024]{2,1,0:T(8,128)(2,1)S(1)}, u32[]{:S(2)}, u32[]{:S(2)}) async-start(bf16[4,128,1024]{2,1,0:T(8,128)(2,1)} %bitcast.10), calls=%async_computation.4 | async-start | bytes 2097152 | tf_op jit(solution)/shard_map/all_to_all | solution.py:49
  243.5 4.2 %collective-permute-start.4 = (f32[2,3072]{1,0:T(2,128)S(1)}, f32[2,3072]{1,0:T(2,128)S(1)}, u32[]{:S(2)}, u32[]{:S(2)}) collective-permute-start(f32[2,3072]{1,0:T(2,128)S(1)} %maximum_maximum_fusion), channel_id=1, source_target_pairs={{0,1},{1,0},{2,3},{3,2},{4,5},{5,4},{6,7},{7,6},{8,9},{9,8},{10,11... | collective-permute-start | bytes 73736 | tf_op jit(solution)/shard_map/ppermute | solution.py:61
  247.8 14.5 %collective-permute-start.5 = (f32[2,3072]{1,0:T(2,128)S(1)}, f32[2,3072]{1,0:T(2,128)S(1)}, u32[]{:S(2)}, u32[]{:S(2)}) collective-permute-start(f32[2,3072]{1,0:T(2,128)S(1)} %fusion.41), channel_id=1, source_target_pairs={{0,2},{1,3},{2,0},{3,1},{4,6},{5,7},{6,4},{7,5},{8,10},{9,11},{10,... | collective-permute-start | bytes 73736 | tf_op jit(solution)/shard_map/ppermute | solution.py:61
  248.1 26.9 %copy-start.11 = (bf16[1024,128]{1,0:T(8,128)(2,1)S(1)}, bf16[1024,128]{1,0:T(8,128)(2,1)}, u32[]{:S(2)}) copy-start(bf16[1024,128]{1,0:T(8,128)(2,1)} %param.9) | copy-start | bytes 786436
  248.1 27.1 %copy-start.16 = (bf16[128]{0:T(256)(128)(2,1)S(1)}, bf16[128]{0:T(256)(128)(2,1)}, u32[]{:S(2)}) copy-start(bf16[128]{0:T(256)(128)(2,1)} %param.12) | copy-start | bytes 772
  258.7 23.7 %all-to-all-start.2 = ((bf16[4,256,512]{2,1,0:T(8,128)(2,1)}), bf16[4,256,512]{2,1,0:T(8,128)(2,1)S(1)}, u32[]{:S(2)}, u32[]{:S(2)}) async-start(bf16[4,256,512]{2,1,0:T(8,128)(2,1)} %broadcast_in_dim.13), calls=%async_computation.3 | async-start | bytes 2097152 | tf_op jit(solution)/shard_map/all_to_all | solution.py:53
  262.3 4.0 %collective-permute-start.6 = (f32[2,3072]{1,0:T(2,128)S(1)}, f32[2,3072]{1,0:T(2,128)S(1)}, u32[]{:S(2)}, u32[]{:S(2)}) collective-permute-start(f32[2,3072]{1,0:T(2,128)S(1)} %fusion.42), channel_id=1, source_target_pairs={{0,4},{1,5},{2,6},{3,7},{4,0},{5,1},{6,2},{7,3},{8,12},{9,13},{10,... | collective-permute-start | bytes 73736 | tf_op jit(solution)/shard_map/ppermute | solution.py:61
  266.4 5.4 %collective-permute-start.7 = (f32[2,3072]{1,0:T(2,128)S(1)}, f32[2,3072]{1,0:T(2,128)S(1)}, u32[]{:S(2)}, u32[]{:S(2)}) collective-permute-start(f32[2,3072]{1,0:T(2,128)S(1)} %add.87), channel_id=1, source_target_pairs={{0,8},{1,9},{2,10},{3,11},{4,12},{5,13},{6,14},{7,15},{8,0},{9,1},... | collective-permute-start | bytes 73736 | tf_op jit(solution)/shard_map/ppermute | solution.py:61
  271.8 1.3 collective-permute-start.8
  273.1 3.8 %collective-permute-start.9 = (f32[2,2048]{1,0:T(2,128)S(1)}, f32[2,2048]{1,0:T(2,128)S(1)}, u32[]{:S(2)}, u32[]{:S(2)}) collective-permute-start(f32[2,2048]{1,0:T(2,128)S(1)} %slice_add_fusion), channel_id=1, source_target_pairs={{0,32},{32,0},{64,96},{96,64},{1,33},{33,1},{65,97},{97,65},{2,34}... | collective-permute-start | bytes 49160 | tf_op jit(solution)/shard_map/ppermute | solution.py:61
  276.9 5.3 %collective-permute-start.10 = (f32[2,2048]{1,0:T(2,128)S(1)}, f32[2,2048]{1,0:T(2,128)S(1)}, u32[]{:S(2)}, u32[]{:S(2)}) collective-permute-start(f32[2,2048]{1,0:T(2,128)S(1)} %add.92), channel_id=1, source_target_pairs={{0,64},{32,96},{64,0},{96,32},{1,65},{33,97},{65,1},{97,33},{2,66}... | collective-permute-start | bytes 49160 | tf_op jit(solution)/shard_map/ppermute | solution.py:61
  283.6 17.7 %all-to-all-start.4 = ((bf16[4,128,1024]{2,1,0:T(8,128)(2,1)}), bf16[4,128,1024]{2,1,0:T(8,128)(2,1)S(1)}, u32[]{:S(2)}, u32[]{:S(2)}) async-start(bf16[4,128,1024]{2,1,0:T(8,128)(2,1)} %broadcast_in_dim.14), calls=%async_computation.5 | async-start | bytes 2097152 | tf_op jit(solution)/shard_map/all_to_all | solution.py:53
  301.5 3.2 %copy-start.13 = (bf16[1024,128]{1,0:T(8,128)(2,1)S(1)}, bf16[1024,128]{1,0:T(8,128)(2,1)}, u32[]{:S(2)}) copy-start(bf16[1024,128]{1,0:T(8,128)(2,1)} %param.10) | copy-start | bytes 786436
Sparse Core Ops, SparseCore 0:
  10.7 60.3 all-gather.1
  93.5 121.3 reduce-scatter.4
  218.6 77.0 reduce-scatter.6

commit v4 on v0

--- a/solution.py
+++ b/solution.py
@@ -71,9 +71,9 @@
     stacked = jnp.concatenate(
         [tokens, ln_gain[None], ln_bias[None], jnp.zeros((6, tokens.shape[1]), tokens.dtype)]
     )
-    gathered = lax.all_to_all(
-        jnp.tile(stacked, (1, sizes["tp"])), "tp", split_axis=1, concat_axis=1, tiled=True
-    )
+    copies = jnp.broadcast_to(stacked[None], (sizes["tp"],) + stacked.shape)
+    gathered = lax.all_to_all(copies, "tp", split_axis=0, concat_axis=0, tiled=True)
+    gathered = jnp.transpose(gathered, (1, 0, 2)).reshape(stacked.shape[0], -1)
     whole_rows = gathered[:frames]
     gain_full, bias_full = gathered[frames], gathered[frames + 1]
     masked_in = apply_blocks(weight_in, blocks_in, jnp.bfloat16)

time: 286 us -> 286 us (level)
  no operation moved by 1% of the time
where the time goes in v4:
time: 286 us; the launch traced here: 285 us
  waiting for transfers between devices  139 us (49%)
  starting transfers between devices  38.8 us (14%)
  matrix products  38.1 us (13%)
  other arithmetic  31 us (11%)
  local copies, waits for them, and re-layouts  23.6 us (8%)
  between operations  14.2 us (5%)
    all_to_all x1, waiting for transfers between devices, on_device(): lax.all_to_all(copies, 'tp', split_axis=0, concat_axis=0, tiled=True)  57.2 us
    reduce_scatter x1, waiting for transfers between devices, on_device(): lax.psum_scatter(partial_out, 'tp', scatter_dimension=0, tiled=True)  40.1 us
    ppermute x7, waiting for transfers between devices, butterfly_sum(): values = values + lax.ppermute(values, axis, perm=perm)  15.4 us
    ppermute x7, starting transfers between devices, butterfly_sum(): values = values + lax.ppermute(values, axis, perm=perm)  14.4 us
    unnamed x38, local copies, waits for them, and re-layouts  14.3 us
    dot_general x2, matrix products, contract_cols(): lax.dot_general(left, right, (((1,), (1,)), ((), ())), preferred_element_...  14.1 us
    all_to_all x2, waiting for transfers between devices, rows_allreduce(): lax.all_to_all(copies, axis, split_axis=0, concat_axis=0, tiled=True)  10.7 us
    dot_general x1, matrix products, on_device(): hidden = jnp.dot(scaled, full_in, preferred_element_type=jnp.float32)  9.98 us
  transfers between devices with their start and end apart: 19, of which 13 were waited for; matrix products, arithmetic and copies ran while one was open for 28% of the time, Pallas kernels for 0%

profile of v4, /device:TPU:0, one launch (start us, length us, event | category | flops | bytes accessed | tf_op | source)
XLA Modules:
  0.0 284.5 jit_solution(16910584035781176260)
XLA Ops:
  7.2 1.7 concatenate.12
  8.9 2.5 broadcast_in_dim.15
  11.4 8.3 %all-to-all-start = ((bf16[16,1032,128]{2,1,0:T(8,128)(2,1)}), bf16[16,1032,128]{2,1,0:T(8,128)(2,1)}, u32[]{:S(2)}, u32[]{:S(2)}) async-start(bf16[16,1032,128]{2,1,0:T(8,128)(2,1)} %broadcast_in_dim.15), calls=%async_computation | async-start | bytes 8454144 | tf_op jit(solution)/shard_map/all_to_all | solution.py:75
  19.8 0.7 all-gather.2.cloned.1.call-update
  20.6 0.3 mul.164
  21.3 0.2 mul.168
  21.5 0.7 copy-done.3
  22.4 1.6 collective-permute-done
  24.0 2.3 broadcast_select_fusion.3
  26.4 2.7 broadcast_select_fusion.1
  29.1 57.2 %all-to-all-done = bf16[16,1032,128]{2,1,0:T(8,128)(2,1)} async-done(((bf16[16,1032,128]{2,1,0:T(8,128)(2,1)}), bf16[16,1032,128]{2,1,0:T(8,128)(2,1)}, u32[]{:S(2)}, u32[]{:S(2)}) %all-to-all-start) | async-done | bytes 4227104 | tf_op jit(solution)/shard_map/all_to_all | solution.py:75
  86.2 3.0 %convert_reduce_fusion = f32[1024]{0:T(1024)S(1)} fusion(bf16[1032,16,128]{2,0,1:T(8,128)(2,1)} %bitcast.2), kind=kLoop, calls=%fused_computation.1 | loop fusion | flops 4193280 | bytes 4198400 | tf_op jit(solution)/shard_map/reduce_sum | solution.py:88
  89.2 3.2 %fusion.5 = f32[1024]{0:T(1024)S(1)} fusion(f32[1024]{0:T(1024)S(1)} %broadcast_multiply_fusion, bf16[1032,16,128]{2,0,1:T(8,128)(2,1)} %bitcast.2), kind=kLoop, calls=%fused_computation.11 | loop fusion | flops 8387584 | bytes 4202496 | tf_op jit(solution)/shard_map/reduce_sum | solution.py:90
  92.4 0.8 slice_convert_fusion.1
  93.3 10.0 %multiply_convert_fusion = (bf16[1024,512]{1,0:T(8,128)(2,1)S(1)}, f32[1024,512]{1,0:T(8,128)}, f32[1024,512]{1,0:T(8,128)}) fusion(bf16[1024,512]{1,0:T(8,128)(2,1)S(1)} %copy-done.4, bf16[1024,512]{1,0:T(8,128)(2,1)S(1)} %get-tuple-element.42, f32[2048]{0:T(1024)S(1)} %bitcast.93, f32[2048]{0:T(1024)S(1)} %bitcast.90, f32[1024]{0:T(1024)S(1)} %add_rsqrt_fusion, ...), kind=kOutput, calls=%fused_computation.34 | convolution fusion | flops 2198339584 | bytes 11558912 | tf_op jit(solution)/shard_map/dot_general | solution.py:94
  103.3 1.0 copy-done.13
  104.3 4.4 %convolution_convert_fusion.1 = bf16[2048,1024]{1,0:T(8,128)(2,1)} fusion(bf16[1024,512]{1,0:T(8,128)(2,1)S(1)} %get-tuple-element.36, bf16[512,1024]{1,0:T(8,128)(2,1)S(1)} %copy-done.6, bf16[512,1024]{1,0:T(8,128)(2,1)S(1)} %copy-done.5), kind=kOutput, calls=%fused_computation.16 | convolution fusion | flops 2153775104 | bytes 7340032 | tf_op jit(solution)/shard_map/dot_general | solution.py:96
  108.7 0.2 reduce-scatter.7.cloned.1.call-start
  108.9 0.4 copy-done.9
  109.4 3.7 %all-gather.2.cloned.1.call-done = bf16[1024,2048]{1,0:T(8,128)(2,1)} async-done(((bf16[1024,128]{1,0:T(8,128)(2,1)}), bf16[1024,2048]{1,0:T(8,128)(2,1)}) %all-gather.2.cloned.1.call-update) | async-done | bytes 4194320 | tf_op jit(solution)/shard_map/all_gather | solution.py:99
  113.1 6.7 %add_convert_fusion.1 = bf16[1024,512]{1,0:T(8,128)(2,1)S(1)} fusion(f32[1024,512]{1,0:T(8,128)} %get-tuple-element.37, f32[1024,512]{1,0:T(8,128)} %get-tuple-element.52, bf16[1024,2048]{1,0:T(8,128)(2,1)} %all-gather.2.cloned.1.call-done, bf16[1024]{0:T(1024)(128)(2,1)S(1)} %convert_element_type.140, bf16[512,1024]{1,0:T(8,128)(2,1)} %get-tuple-element.41, ...), kind=kOutput, calls=%fused_computation.31 | convolution fusion | flops 2161115136 | bytes 11536384 | tf_op jit(solution)/shard_map/dot_general | solution.py:25
  119.8 7.4 %fusion.2 = (f32[1024]{0:T(1024)S(1)}, f32[2048]{0:T(1024)S(1)}, f32[1024]{0:T(1024)S(1)}, f32[2048]{0:T(1024)S(1)}, bf16[1024,2048]{1,0:T(8,128)(2,1)}) fusion(f32[2048]{0:T(1024)S(1)} %bitcast.91, bf16[1024,512]{1,0:T(8,128)(2,1)S(1)} %add_convert_fusion.1, bf16[1024,512]{1,0:T(8,128)(2,1)S(1)} %copy-done.4, bf16[1024,512]{1,0:T(8,128)(2,1)S(1)} %get-tuple-element.42, ...), kind=kOutput, calls=%fused_computation.8 | convolution fusion | flops 2176837632 | bytes 11575296 | tf_op jit(solution)/shard_map/dot_general | solution.py:25
  127.2 6.4 %copy.24 = bf16[1024,2048]{0,1:T(8,128)(2,1)} copy(bf16[1024,2048]{1,0:T(8,128)(2,1)} %get-tuple-element.53) | data formatting | bytes 8388608
  133.6 1.2 copy-done.14
  134.8 4.7 %fusion.11 = bf16[512,2048]{1,0:T(8,128)(2,1)S(1)} fusion(bf16[1024,512]{1,0:T(8,128)(2,1)S(1)} %copy-done.14, bf16[1024,2048]{1,0:T(8,128)(2,1)} %all-gather.2.cloned.1.call-done, bf16[1024]{0:T(1024)(128)(2,1)S(1)} %convert_element_type.140), kind=kOutput, calls=%fused_computation.23 | convolution fusion | flops 2150629376 | bytes 7342080 | tf_op jit(solution)/shard_map/dot_general | solution.py:19
  139.7 1.0 copy-done.16
  140.7 5.0 %convolution_convert_fusion.2 = bf16[2048,512]{1,0:T(8,128)(2,1)S(1)} fusion(bf16[1024,512]{1,0:T(8,128)(2,1)S(1)} %copy-done.16, f32[2048]{0:T(1024)S(1)} %bitcast.94, f32[2048]{0:T(1024)S(1)} %bitcast.92, f32[1024]{0:T(1024)S(1)} %add_rsqrt_fusion, f32[1024]{0:T(1024)S(1)} %broadcast_multiply_fusion, bf16[1032,16,128]{2,0,1:T(8,128)(2,1)} %bitcast.2), kind=kOutput, calls=%fused_computation.22 | convolution fusion | flops 2161115136 | bytes 7364608 | tf_op jit(solution)/shard_map/dot_general | solution.py:19
  145.8 1.3 copy-done
  147.1 1.0 constant_dynamic-slice_fusion.3
  148.1 2.8 convert_add_fusion
  150.9 0.2 collective-permute-done.2
  151.1 2.5 convert_add_fusion.1
  153.6 40.1 %reduce-scatter.5.cloned.1.call-done = bf16[128,1024]{1,0:T(8,128)(2,1)} async-done(((bf16[2048,1024]{1,0:T(8,128)(2,1)}), bf16[128,1024]{1,0:T(8,128)(2,1)}) %reduce-scatter.5.cloned.1.call-update) | async-done | bytes 262160 | tf_op jit(solution)/shard_map/reduce_scatter | solution.py:101
  193.7 1.0 convert_bitcast_fusion.1
  194.7 4.3 %all-to-all-start.1 = ((bf16[4,256,512]{2,1,0:T(8,128)(2,1)}), bf16[4,256,512]{2,1,0:T(8,128)(2,1)S(1)}, u32[]{:S(2)}, u32[]{:S(2)}) async-start(bf16[4,256,512]{2,1,0:T(8,128)(2,1)} %bitcast.6), calls=%async_computation.2 | async-start | bytes 2097152 | tf_op jit(solution)/shard_map/all_to_all | solution.py:49
  199.1 1.3 collective-permute-start.4
  200.4 2.6 collective-permute-done.4
  203.0 2.7 collective-permute-start.5
  205.8 6.8 %all-to-all-done.1 = bf16[4,256,512]{2,1,0:T(8,128)(2,1)S(1)} async-done(((bf16[4,256,512]{2,1,0:T(8,128)(2,1)}), bf16[4,256,512]{2,1,0:T(8,128)(2,1)S(1)}, u32[]{:S(2)}, u32[]{:S(2)}) %all-to-all-start.1) | async-done | bytes 1048608 | tf_op jit(solution)/shard_map/all_to_all | solution.py:49
  212.6 3.5 %all-to-all-start.3 = ((bf16[4,128,1024]{2,1,0:T(8,128)(2,1)}), bf16[4,128,1024]{2,1,0:T(8,128)(2,1)S(1)}, u32[]{:S(2)}, u32[]{:S(2)}) async-start(bf16[4,128,1024]{2,1,0:T(8,128)(2,1)} %bitcast.8), calls=%async_computation.4 | async-start | bytes 2097152 | tf_op jit(solution)/shard_map/all_to_all | solution.py:49
  216.1 1.6 collective-permute-start.6
  217.7 2.6 collective-permute-done.6
  220.3 2.7 collective-permute-start.7
  223.0 2.9 %collective-permute-done.7 = f32[2,3072]{1,0:T(2,128)S(1)} collective-permute-done((f32[2,3072]{1,0:T(2,128)S(1)}, f32[2,3072]{1,0:T(2,128)S(1)}, u32[]{:S(2)}, u32[]{:S(2)}) %collective-permute-start.7) | collective-permute-done | bytes 24608 | tf_op jit(solution)/shard_map/ppermute | solution.py:61
  226.3 0.9 collective-permute-done.8
  227.2 2.4 collective-permute-start.9
  229.6 0.2 reduce_sum.80
  229.9 1.1 broadcast_in_dim.16
  230.9 4.2 %all-to-all-start.2 = ((bf16[4,256,512]{2,1,0:T(8,128)(2,1)}), bf16[4,256,512]{2,1,0:T(8,128)(2,1)S(1)}, u32[]{:S(2)}, u32[]{:S(2)}) async-start(bf16[4,256,512]{2,1,0:T(8,128)(2,1)} %broadcast_in_dim.16), calls=%async_computation.3 | async-start | bytes 2097152 | tf_op jit(solution)/shard_map/all_to_all | solution.py:53
  235.1 5.5 %fusion.6 = f32[1024,2048]{1,0:T(8,128)} fusion(f32[1024]{0:T(1024)S(1)} %add_rsqrt_fusion, f32[1024]{0:T(1024)S(1)} %broadcast_multiply_fusion, bf16[1032,16,128]{2,0,1:T(8,128)(2,1)} %bitcast.2), kind=kLoop, calls=%fused_computation.13 | loop fusion | flops 6291456 | bytes 12591104 | tf_op jit(solution)/shard_map/mul | solution.py:91
  240.6 3.6 %collective-permute-start.10 = (f32[2,2048]{1,0:T(2,128)S(1)}, f32[2,2048]{1,0:T(2,128)S(1)}, u32[]{:S(2)}, u32[]{:S(2)}) collective-permute-start(f32[2,2048]{1,0:T(2,128)S(1)} %add.85), channel_id=1, source_target_pairs={{0,64},{32,96},{64,0},{96,32},{1,65},{33,97},{65,1},{97,33},{2,66}... | collective-permute-start | bytes 49160 | tf_op jit(solution)/shard_map/ppermute | solution.py:61
  244.3 6.4 %collective-permute-done.10 = f32[2,2048]{1,0:T(2,128)S(1)} collective-permute-done((f32[2,2048]{1,0:T(2,128)S(1)}, f32[2,2048]{1,0:T(2,128)S(1)}, u32[]{:S(2)}, u32[]{:S(2)}) %collective-permute-start.10) | collective-permute-done | bytes 16416 | tf_op jit(solution)/shard_map/ppermute | solution.py:61
  250.8 1.1 broadcast_in_dim.17
  251.9 3.5 %all-to-all-start.4 = ((bf16[4,128,1024]{2,1,0:T(8,128)(2,1)}), bf16[4,128,1024]{2,1,0:T(8,128)(2,1)S(1)}, u32[]{:S(2)}, u32[]{:S(2)}) async-start(bf16[4,128,1024]{2,1,0:T(8,128)(2,1)} %broadcast_in_dim.17), calls=%async_computation.5 | async-start | bytes 2097152 | tf_op jit(solution)/shard_map/all_to_all | solution.py:53
  255.5 0.5 fusion.25
  256.1 0.8 copy.23
  256.9 0.3 mul.187
  257.3 1.8 bitcast_multiply_fusion.1
  259.0 10.7 %all-to-all-done.4 = bf16[4,128,1024]{2,1,0:T(8,128)(2,1)S(1)} async-done(((bf16[4,128,1024]{2,1,0:T(8,128)(2,1)}), bf16[4,128,1024]{2,1,0:T(8,128)(2,1)S(1)}, u32[]{:S(2)}, u32[]{:S(2)}) %all-to-all-start.4) | async-done | bytes 1048608 | tf_op jit(solution)/shard_map/all_to_all | solution.py:53
  269.7 0.2 mul.190
  269.9 2.1 bitcast_multiply_fusion
  272.0 2.5 reduce-scatter.7.cloned.1.call-done
  274.5 1.1 copy.25
  275.7 2.4 add_convert_fusion.4
  (70 shorter events, 1.8 us)
Async XLA Ops:
  11.4 9.1 %copy-start.10 = (s32[8,4]{0,1:T(4,128)S(1)}, s32[8,4]{0,1:T(4,128)}, u32[]{:S(2)}) copy-start(s32[8,4]{0,1:T(4,128)} %param.16) | copy-start | bytes 388
  11.4 9.6 %copy-start.2 = (bf16[1024,512]{1,0:T(8,128)(2,1)S(1)}, bf16[1024,512]{1,0:T(8,128)(2,1)}, u32[]{:S(2)}) copy-start(bf16[1024,512]{1,0:T(8,128)(2,1)} %param.14) | copy-start | bytes 3145732
  11.4 74.8 %all-to-all-start = ((bf16[16,1032,128]{2,1,0:T(8,128)(2,1)}), bf16[16,1032,128]{2,1,0:T(8,128)(2,1)}, u32[]{:S(2)}, u32[]{:S(2)}) async-start(bf16[16,1032,128]{2,1,0:T(8,128)(2,1)} %broadcast_in_dim.15), calls=%async_computation | async-start | bytes 8454144 | tf_op jit(solution)/shard_map/all_to_all | solution.py:75
  19.7 93.4 %all-gather.2.cloned.1.call-start = ((), (), s32[]{:S(2)}) async-start(), calls=%async_computation.7 | async-start | bytes 4456448 | tf_op jit(solution)/shard_map/all_gather | solution.py:99
  20.5 173.2 %reduce-scatter.5.cloned.1.call-start = ((), (), s32[]{:S(2)}) async-start(), calls=%async_computation.8 | async-start | bytes 4456448 | tf_op jit(solution)/shard_map/reduce_scatter | solution.py:101
  20.6 0.7 copy-start.11
  21.0 1.2 copy-start.3
  21.2 2.9 %collective-permute-start = (bf16[1024,512]{1,0:T(8,128)(2,1)S(1)}, bf16[1024,512]{1,0:T(8,128)(2,1)}, u32[]{:S(2)}, u32[]{:S(2)}) collective-permute-start(bf16[1024,512]{1,0:T(8,128)(2,1)S(1)} %bitcast_multiply_fusion.3), channel_id=1, source_target_pairs={{0,16},{16,0},{1,17},{17,1},{2,18},{18,2},{3,19},{19,3},{4,20},{20... | collective-permute-start | bytes 3145736 | tf_op jit(solution)/shard_map/ppermute | solution.py:31
  22.3 4.0 %collective-permute-start.1 = (bf16[512,1024]{1,0:T(8,128)(2,1)S(1)}, bf16[512,1024]{1,0:T(8,128)(2,1)}, u32[]{:S(2)}, u32[]{:S(2)}) collective-permute-start(bf16[512,1024]{1,0:T(8,128)(2,1)S(1)} %bitcast_multiply_fusion.2), channel_id=1, source_target_pairs={{0,16},{16,0},{1,17},{17,1},{2,18},{18,2},{3,19},{19,3},{4,20},{20... | collective-permute-start | bytes 3145736 | tf_op jit(solution)/shard_map/ppermute | solution.py:31
  89.2 4.1 %copy-start.4 = (bf16[1024,512]{1,0:T(8,128)(2,1)S(1)}, bf16[1024,512]{1,0:T(8,128)(2,1)}, u32[]{:S(2)}) copy-start(bf16[1024,512]{1,0:T(8,128)(2,1)} %get-tuple-element.43) | copy-start | bytes 3145732
  93.3 11.0 %copy-start.5 = (bf16[512,1024]{1,0:T(8,128)(2,1)S(1)}, bf16[512,1024]{1,0:T(8,128)(2,1)}, u32[]{:S(2)}) copy-start(bf16[512,1024]{1,0:T(8,128)(2,1)} %get-tuple-element.40) | copy-start | bytes 3145732
  93.3 11.0 %copy-start.6 = (bf16[512,1024]{1,0:T(8,128)(2,1)S(1)}, bf16[512,1024]{1,0:T(8,128)(2,1)}, u32[]{:S(2)}) copy-start(bf16[512,1024]{1,0:T(8,128)(2,1)} %get-tuple-element.41) | copy-start | bytes 3145732
  103.3 1.0 copy-start.13
  108.7 0.7 copy-start.9
  108.7 165.8 %reduce-scatter.7.cloned.1.call-start = ((), (), s32[]{:S(2)}) async-start(), calls=%async_computation.9 | async-start | bytes 4456448
  119.8 7.4 %copy-start.15 = (bf16[1024,512]{1,0:T(8,128)(2,1)}, bf16[1024,512]{1,0:T(8,128)(2,1)S(1)}, u32[]{:S(2)}) copy-start(bf16[1024,512]{1,0:T(8,128)(2,1)S(1)} %add_convert_fusion.1) | copy-start | bytes 3145732
  133.6 1.2 copy-start.14
  139.5 1.2 copy-start.16
  139.6 8.5 %collective-permute-start.3 = (bf16[512,1024]{1,0:T(8,128)(2,1)S(1)}, bf16[512,1024]{1,0:T(8,128)(2,1)}, u32[]{:S(2)}, u32[]{:S(2)}) collective-permute-start(bf16[512,1024]{1,0:T(8,128)(2,1)S(1)} %constant_dynamic-slice_fusion.2), channel_id=1, source_target_pairs={{0,16},{16,0},{1,17},{17,1},{2,18},{18,2},{3,19},{19,3},{4,20},{20... | collective-permute-start | bytes 3145736 | tf_op jit(solution)/shard_map/ppermute | solution.py:43
  145.7 1.3 copy-start
  148.1 3.0 %collective-permute-start.2 = (bf16[1024,512]{1,0:T(8,128)(2,1)}, bf16[1024,512]{1,0:T(8,128)(2,1)}, u32[]{:S(2)}, u32[]{:S(2)}) collective-permute-start(bf16[1024,512]{1,0:T(8,128)(2,1)} %constant_dynamic-slice_fusion.3), channel_id=1, source_target_pairs={{0,16},{16,0},{1,17},{17,1},{2,18},{18,2},{3,19},{19,3},{4,20},{20... | collective-permute-start | bytes 3145736 | tf_op jit(solution)/shard_map/ppermute | solution.py:43
  148.1 3.0 %copy-start.1 = (bf16[2048,512]{1,0:T(8,128)(2,1)S(1)}, bf16[2048,512]{1,0:T(8,128)(2,1)}, u32[]{:S(2)}) copy-start(bf16[2048,512]{1,0:T(8,128)(2,1)} %copy-done) | copy-start | bytes 6291460
  194.7 31.3 %copy-start.12 = (bf16[128]{0:T(256)(128)(2,1)S(1)}, bf16[128]{0:T(256)(128)(2,1)}, u32[]{:S(2)}) copy-start(bf16[128]{0:T(256)(128)(2,1)} %param.12) | copy-start | bytes 772
  194.7 31.3 %copy-start.7 = (bf16[1024,128]{1,0:T(8,128)(2,1)S(1)}, bf16[1024,128]{1,0:T(8,128)(2,1)}, u32[]{:S(2)}) copy-start(bf16[1024,128]{1,0:T(8,128)(2,1)} %param.9) | copy-start | bytes 786436
  194.7 17.8 %all-to-all-start.1 = ((bf16[4,256,512]{2,1,0:T(8,128)(2,1)}), bf16[4,256,512]{2,1,0:T(8,128)(2,1)S(1)}, u32[]{:S(2)}, u32[]{:S(2)}) async-start(bf16[4,256,512]{2,1,0:T(8,128)(2,1)} %bitcast.6), calls=%async_computation.2 | async-start | bytes 2097152 | tf_op jit(solution)/shard_map/all_to_all | solution.py:49
  199.1 3.9 %collective-permute-start.4 = (f32[2,3072]{1,0:T(2,128)S(1)}, f32[2,3072]{1,0:T(2,128)S(1)}, u32[]{:S(2)}, u32[]{:S(2)}) collective-permute-start(f32[2,3072]{1,0:T(2,128)S(1)} %maximum_maximum_fusion), channel_id=1, source_target_pairs={{0,1},{1,0},{2,3},{3,2},{4,5},{5,4},{6,7},{7,6},{8,9},{9,8},{10,11... | collective-permute-start | bytes 73736 | tf_op jit(solution)/shard_map/ppermute | solution.py:61
  203.0 13.1 %collective-permute-start.5 = (f32[2,3072]{1,0:T(2,128)S(1)}, f32[2,3072]{1,0:T(2,128)S(1)}, u32[]{:S(2)}, u32[]{:S(2)}) collective-permute-start(f32[2,3072]{1,0:T(2,128)S(1)} %fusion.39), channel_id=1, source_target_pairs={{0,2},{1,3},{2,0},{3,1},{4,6},{5,7},{6,4},{7,5},{8,10},{9,11},{10,... | collective-permute-start | bytes 73736 | tf_op jit(solution)/shard_map/ppermute | solution.py:61
  212.6 17.3 %all-to-all-start.3 = ((bf16[4,128,1024]{2,1,0:T(8,128)(2,1)}), bf16[4,128,1024]{2,1,0:T(8,128)(2,1)S(1)}, u32[]{:S(2)}, u32[]{:S(2)}) async-start(bf16[4,128,1024]{2,1,0:T(8,128)(2,1)} %bitcast.8), calls=%async_computation.4 | async-start | bytes 2097152 | tf_op jit(solution)/shard_map/all_to_all | solution.py:49
  216.1 4.1 %collective-permute-start.6 = (f32[2,3072]{1,0:T(2,128)S(1)}, f32[2,3072]{1,0:T(2,128)S(1)}, u32[]{:S(2)}, u32[]{:S(2)}) collective-permute-start(f32[2,3072]{1,0:T(2,128)S(1)} %fusion.40), channel_id=1, source_target_pairs={{0,4},{1,5},{2,6},{3,7},{4,0},{5,1},{6,2},{7,3},{8,12},{9,13},{10,... | collective-permute-start | bytes 73736 | tf_op jit(solution)/shard_map/ppermute | solution.py:61
  220.3 5.6 %collective-permute-start.7 = (f32[2,3072]{1,0:T(2,128)S(1)}, f32[2,3072]{1,0:T(2,128)S(1)}, u32[]{:S(2)}, u32[]{:S(2)}) collective-permute-start(f32[2,3072]{1,0:T(2,128)S(1)} %add.80), channel_id=1, source_target_pairs={{0,8},{1,9},{2,10},{3,11},{4,12},{5,13},{6,14},{7,15},{8,0},{9,1},... | collective-permute-start | bytes 73736 | tf_op jit(solution)/shard_map/ppermute | solution.py:61
  225.9 1.3 collective-permute-start.8
  227.2 13.4 %collective-permute-start.9 = (f32[2,2048]{1,0:T(2,128)S(1)}, f32[2,2048]{1,0:T(2,128)S(1)}, u32[]{:S(2)}, u32[]{:S(2)}) collective-permute-start(f32[2,2048]{1,0:T(2,128)S(1)} %slice_add_fusion), channel_id=1, source_target_pairs={{0,32},{32,0},{64,96},{96,64},{1,33},{33,1},{65,97},{97,65},{2,34}... | collective-permute-start | bytes 49160 | tf_op jit(solution)/shard_map/ppermute | solution.py:61
  230.9 19.9 %all-to-all-start.2 = ((bf16[4,256,512]{2,1,0:T(8,128)(2,1)}), bf16[4,256,512]{2,1,0:T(8,128)(2,1)S(1)}, u32[]{:S(2)}, u32[]{:S(2)}) async-start(bf16[4,256,512]{2,1,0:T(8,128)(2,1)} %broadcast_in_dim.16), calls=%async_computation.3 | async-start | bytes 2097152 | tf_op jit(solution)/shard_map/all_to_all | solution.py:53
  240.6 10.0 %collective-permute-start.10 = (f32[2,2048]{1,0:T(2,128)S(1)}, f32[2,2048]{1,0:T(2,128)S(1)}, u32[]{:S(2)}, u32[]{:S(2)}) collective-permute-start(f32[2,2048]{1,0:T(2,128)S(1)} %add.85), channel_id=1, source_target_pairs={{0,64},{32,96},{64,0},{96,32},{1,65},{33,97},{65,1},{97,33},{2,66}... | collective-permute-start | bytes 49160 | tf_op jit(solution)/shard_map/ppermute | solution.py:61
  251.9 17.7 %all-to-all-start.4 = ((bf16[4,128,1024]{2,1,0:T(8,128)(2,1)}), bf16[4,128,1024]{2,1,0:T(8,128)(2,1)S(1)}, u32[]{:S(2)}, u32[]{:S(2)}) async-start(bf16[4,128,1024]{2,1,0:T(8,128)(2,1)} %broadcast_in_dim.17), calls=%async_computation.5 | async-start | bytes 2097152 | tf_op jit(solution)/shard_map/all_to_all | solution.py:53
  269.9 5.8 %copy-start.8 = (bf16[1024,128]{1,0:T(8,128)(2,1)S(1)}, bf16[1024,128]{1,0:T(8,128)(2,1)}, u32[]{:S(2)}) copy-start(bf16[1024,128]{1,0:T(8,128)(2,1)} %param.10) | copy-start | bytes 786436
Sparse Core Ops, SparseCore 0:
  22.7 90.3 all-gather.1
  116.4 77.2 reduce-scatter.4
  197.4 77.0 reduce-scatter.6

commit v5 on v0

--- a/solution.py
+++ b/solution.py
@@ -129,8 +129,11 @@
     shard_out = pair_scatter(term_out, 1)
     shard_in, shard_out, branch = lax.optimization_barrier((shard_in, shard_out, branch))
     block_out = (tokens.astype(jnp.float32) + branch).astype(jnp.bfloat16)
-    shard_in = rows_allreduce(shard_in, "rep", sizes["rep"])
-    shard_out = rows_allreduce(shard_out, "rep", sizes["rep"])
+    rows_in = shard_in.shape[0]
+    paired = jnp.concatenate([shard_in, shard_out.reshape(rows_in, -1)], axis=1)
+    paired = rows_allreduce(paired, "rep", sizes["rep"])
+    shard_out = paired[:, shard_in.shape[1]:].reshape(shard_out.shape)
+    shard_in = paired[:, : shard_in.shape[1]]
     grad_in = apply_blocks(shard_in, blocks_in, jnp.float32)
     grad_out = apply_blocks(shard_out, blocks_out, jnp.float32)
     grad_in, grad_out, back_normed = lax.optimization_barrier((grad_in, grad_out, back_normed))

time: 286 us -> 286 us (level)
  starting transfers between devices: 38.8 us -> 31 us
  waiting for transfers between devices: 139 us -> 143 us
    all_to_all x2 -> x1, waiting for transfers between devices: 10.7 us -> 0.01 us  [rows_allreduce(): lax.all_to_all(copies, axis, split_axis=0, concat_axis=0, tiled=True)]
    ppermute x7, waiting for transfers between devices: 15.4 us -> 24.2 us  [butterfly_sum(): values = values + lax.ppermute(values, axis, perm=perm)]
    unnamed x4, waiting for transfers between devices: 3.23 us -> 9.27 us
    all_to_all x2 -> x1, starting transfers between devices: 7.69 us -> 3.63 us  [rows_allreduce(): lax.all_to_all(copies, axis, split_axis=0, concat_axis=0, tiled=True)]
    all_to_all x2 -> x1, starting transfers between devices: 7.86 us -> 4.36 us  [rows_allreduce(): lax.all_to_all(term.astype(jnp.bfloat16), axis, split_axis=0, concat_axis...]
    unnamed x38 -> x42, local copies, waits for them, and re-layouts: 14.3 us -> 15.7 us
    all_to_all x2 -> x1, waiting for transfers between devices: 6.81 us -> 5.85 us  [rows_allreduce(): lax.all_to_all(term.astype(jnp.bfloat16), axis, split_axis=0, concat_axis...]
  transfers between devices with their start and end apart: 19 -> 17, of which waited for: 13 -> 11; matrix products, arithmetic and copies ran while one was open for 28% -> 29% of each run, Pallas kernels for 0% -> 0%
where the time goes in v5:
time: 286 us; the launch traced here: 285 us
  waiting for transfers between devices  143 us (50%)
  matrix products  38.1 us (13%)
  other arithmetic  32.2 us (11%)
  starting transfers between devices  31 us (11%)
  local copies, waits for them, and re-layouts  26.4 us (9%)
  between operations  14.2 us (5%)
    all_to_all x1, waiting for transfers between devices, on_device(): lax.all_to_all(jnp.tile(stacked, (1, sizes['tp'])), 'tp', split_axis=1, c...  57.2 us
    reduce_scatter x1, waiting for transfers between devices, on_device(): lax.psum_scatter(partial_out, 'tp', scatter_dimension=0, tiled=True)  41 us
    ppermute x7, waiting for transfers between devices, butterfly_sum(): values = values + lax.ppermute(values, axis, perm=perm)  24.2 us
    unnamed x42, local copies, waits for them, and re-layouts  15.7 us
    ppermute x7, starting transfers between devices, butterfly_sum(): values = values + lax.ppermute(values, axis, perm=perm)  14.1 us
    dot_general x2, matrix products, contract_cols(): lax.dot_general(left, right, (((1,), (1,)), ((), ())), preferred_element_...  14.1 us
    dot_general x1, matrix products, on_device(): hidden = jnp.dot(scaled, full_in, preferred_element_type=jnp.float32)  9.96 us
    dot_general x2, matrix products, contract_rows(): lax.dot_general(left, right, (((0,), (0,)), ((), ())), preferred_element_...  9.69 us
  transfers between devices with their start and end apart: 17, of which 11 were waited for; matrix products, arithmetic and copies ran while one was open for 29% of the time, Pallas kernels for 0%

profile of v5, /device:TPU:0, one launch (start us, length us, event | category | flops | bytes accessed | tf_op | source)
XLA Modules:
  0.0 284.8 jit_solution(10023207382230018043)
XLA Ops:
  7.2 1.7 concatenate.21
  8.9 2.5 tile.2
  11.4 8.3 %all-to-all-start = ((bf16[1032,16,128]{2,0,1:T(8,128)(2,1)}), bf16[1032,16,128]{2,0,1:T(8,128)(2,1)}, u32[]{:S(2)}, u32[]{:S(2)}) async-start(bf16[1032,16,128]{2,0,1:T(8,128)(2,1)} %tile.2), calls=%async_computation | async-start | bytes 8454144 | tf_op jit(solution)/shard_map/all_to_all | solution.py:74
  19.8 0.7 all-gather.2.cloned.1.call-update
  20.6 0.3 mul.164
  21.3 0.2 mul.168
  21.5 0.7 copy-done.5
  22.5 1.6 collective-permute-done
  24.0 2.3 broadcast_select_fusion.3
  26.4 2.7 broadcast_select_fusion.1
  29.1 57.2 %all-to-all-done = bf16[1032,16,128]{2,0,1:T(8,128)(2,1)} async-done(((bf16[1032,16,128]{2,0,1:T(8,128)(2,1)}), bf16[1032,16,128]{2,0,1:T(8,128)(2,1)}, u32[]{:S(2)}, u32[]{:S(2)}) %all-to-all-start) | async-done | bytes 4227104 | tf_op jit(solution)/shard_map/all_to_all | solution.py:74
  86.2 3.0 %convert_reduce_fusion = f32[1024]{0:T(1024)S(1)} fusion(bf16[1032,16,128]{2,0,1:T(8,128)(2,1)} %all-to-all-done), kind=kLoop, calls=%fused_computation.1 | loop fusion | flops 4193280 | bytes 4198400 | tf_op jit(solution)/shard_map/reduce_sum | solution.py:88
  89.2 3.2 %fusion.5 = f32[1024]{0:T(1024)S(1)} fusion(f32[1024]{0:T(1024)S(1)} %broadcast_multiply_fusion, bf16[1032,16,128]{2,0,1:T(8,128)(2,1)} %all-to-all-done), kind=kLoop, calls=%fused_computation.11 | loop fusion | flops 8387584 | bytes 4202496 | tf_op jit(solution)/shard_map/reduce_sum | solution.py:90
  92.4 0.8 slice_convert_fusion.1
  93.3 10.0 %multiply_convert_fusion = (bf16[1024,512]{1,0:T(8,128)(2,1)S(1)}, f32[1024,512]{1,0:T(8,128)}, f32[1024,512]{1,0:T(8,128)}) fusion(bf16[1024,512]{1,0:T(8,128)(2,1)S(1)} %copy-done.6, bf16[1024,512]{1,0:T(8,128)(2,1)S(1)} %get-tuple-element.44, f32[2048]{0:T(1024)S(1)} %bitcast.89, f32[2048]{0:T(1024)S(1)} %bitcast.86, f32[1024]{0:T(1024)S(1)} %add_rsqrt_fusion, ...), kind=kOutput, calls=%fused_computation.36 | convolution fusion | flops 2198339584 | bytes 11558912 | tf_op jit(solution)/shard_map/dot_general | solution.py:94
  103.3 1.0 copy-done.15
  104.3 4.4 %convolution_convert_fusion.1 = bf16[2048,1024]{1,0:T(8,128)(2,1)} fusion(bf16[1024,512]{1,0:T(8,128)(2,1)S(1)} %get-tuple-element.36, bf16[512,1024]{1,0:T(8,128)(2,1)S(1)} %copy-done.8, bf16[512,1024]{1,0:T(8,128)(2,1)S(1)} %copy-done.7), kind=kOutput, calls=%fused_computation.16 | convolution fusion | flops 2153775104 | bytes 7340032 | tf_op jit(solution)/shard_map/dot_general | solution.py:96
  108.7 0.2 reduce-scatter.7.cloned.1.call-start
  108.9 0.4 copy-done.11
  109.4 3.7 %all-gather.2.cloned.1.call-done = bf16[1024,2048]{1,0:T(8,128)(2,1)} async-done(((bf16[1024,128]{1,0:T(8,128)(2,1)}), bf16[1024,2048]{1,0:T(8,128)(2,1)}) %all-gather.2.cloned.1.call-update) | async-done | bytes 4194320 | tf_op jit(solution)/shard_map/all_gather | solution.py:99
  113.1 6.7 %add_convert_fusion.1 = bf16[1024,512]{1,0:T(8,128)(2,1)S(1)} fusion(f32[1024,512]{1,0:T(8,128)} %get-tuple-element.37, f32[1024,512]{1,0:T(8,128)} %get-tuple-element.54, bf16[1024,2048]{1,0:T(8,128)(2,1)} %all-gather.2.cloned.1.call-done, bf16[1024]{0:T(1024)(128)(2,1)S(1)} %convert_element_type.124, bf16[512,1024]{1,0:T(8,128)(2,1)} %get-tuple-element.43, ...), kind=kOutput, calls=%fused_computation.33 | convolution fusion | flops 2161115136 | bytes 11536384 | tf_op jit(solution)/shard_map/dot_general | solution.py:25
  119.8 7.4 %fusion.2 = (f32[1024]{0:T(1024)S(1)}, f32[2048]{0:T(1024)S(1)}, f32[1024]{0:T(1024)S(1)}, f32[2048]{0:T(1024)S(1)}, bf16[1024,2048]{1,0:T(8,128)(2,1)}) fusion(f32[2048]{0:T(1024)S(1)} %bitcast.87, bf16[1024,512]{1,0:T(8,128)(2,1)S(1)} %add_convert_fusion.1, bf16[1024,512]{1,0:T(8,128)(2,1)S(1)} %copy-done.6, bf16[1024,512]{1,0:T(8,128)(2,1)S(1)} %get-tuple-element.44, ...), kind=kOutput, calls=%fused_computation.8 | convolution fusion | flops 2176837632 | bytes 11575296 | tf_op jit(solution)/shard_map/dot_general | solution.py:25
  127.2 6.4 %copy.24 = bf16[1024,2048]{0,1:T(8,128)(2,1)} copy(bf16[1024,2048]{1,0:T(8,128)(2,1)} %get-tuple-element.55) | data formatting | bytes 8388608
  133.6 1.2 copy-done.16
  134.8 4.7 %fusion.11 = bf16[512,2048]{1,0:T(8,128)(2,1)S(1)} fusion(bf16[1024,512]{1,0:T(8,128)(2,1)S(1)} %copy-done.16, bf16[1024,2048]{1,0:T(8,128)(2,1)} %all-gather.2.cloned.1.call-done, bf16[1024]{0:T(1024)(128)(2,1)S(1)} %convert_element_type.124), kind=kOutput, calls=%fused_computation.23 | convolution fusion | flops 2150629376 | bytes 7342080 | tf_op jit(solution)/shard_map/dot_general | solution.py:19
  139.7 1.0 copy-done.18
  140.7 5.0 %convolution_convert_fusion.2 = bf16[2048,512]{1,0:T(8,128)(2,1)S(1)} fusion(bf16[1024,512]{1,0:T(8,128)(2,1)S(1)} %copy-done.18, f32[2048]{0:T(1024)S(1)} %bitcast.90, f32[2048]{0:T(1024)S(1)} %bitcast.88, f32[1024]{0:T(1024)S(1)} %add_rsqrt_fusion, f32[1024]{0:T(1024)S(1)} %broadcast_multiply_fusion, bf16[1032,16,128]{2,0,1:T(8,128)(2,1)} %all-to-all-done), kind=kOutput, calls=%fused_computation.22 | convolution fusion | flops 2161115136 | bytes 7364608 | tf_op jit(solution)/shard_map/dot_general | solution.py:19
  145.7 1.3 copy-done.1
  147.0 1.0 constant_dynamic-slice_fusion.3
  148.1 1.3 collective-permute-start.4
  149.4 1.7 convert_add_fusion
  151.1 1.5 convert_add_fusion.1
  152.6 41.0 %reduce-scatter.5.cloned.1.call-done = bf16[128,1024]{1,0:T(8,128)(2,1)} async-done(((bf16[2048,1024]{1,0:T(8,128)(2,1)}), bf16[128,1024]{1,0:T(8,128)(2,1)}) %reduce-scatter.5.cloned.1.call-update) | async-done | bytes 262160 | tf_op jit(solution)/shard_map/reduce_scatter | solution.py:101
  193.7 1.8 convert_bitcast_fusion.1
  195.5 0.4 concatenate.25
  195.9 1.6 pad_maximum_fusion.2
  197.5 4.4 %all-to-all-start.1 = ((bf16[4,256,1024]{2,1,0:T(8,128)(2,1)}), bf16[4,256,1024]{2,1,0:T(8,128)(2,1)S(1)}, u32[]{:S(2)}, u32[]{:S(2)}) async-start(bf16[4,256,1024]{2,1,0:T(8,128)(2,1)} %pad_maximum_fusion.2), calls=%async_computation.2 | async-start | bytes 4194304 | tf_op jit(solution)/shard_map/all_to_all | solution.py:49
  201.9 2.9 %collective-permute-start.5 = (f32[2,3072]{1,0:T(2,128)S(1)}, f32[2,3072]{1,0:T(2,128)S(1)}, u32[]{:S(2)}, u32[]{:S(2)}) collective-permute-start(f32[2,3072]{1,0:T(2,128)S(1)} %fusion.40), channel_id=1, source_target_pairs={{0,2},{1,3},{2,0},{3,1},{4,6},{5,7},{6,4},{7,5},{8,10},{9,11},{10,... | collective-permute-start | bytes 73736 | tf_op jit(solution)/shard_map/ppermute | solution.py:61
  204.8 2.7 collective-permute-done.5
  207.6 1.3 collective-permute-start.6
  208.8 2.8 collective-permute-done.6
  211.7 2.7 collective-permute-start.7
  214.4 3.0 %collective-permute-done.7 = f32[2,3072]{1,0:T(2,128)S(1)} collective-permute-done((f32[2,3072]{1,0:T(2,128)S(1)}, f32[2,3072]{1,0:T(2,128)S(1)}, u32[]{:S(2)}, u32[]{:S(2)}) %collective-permute-start.7) | collective-permute-done | bytes 24608 | tf_op jit(solution)/shard_map/ppermute | solution.py:61
  217.8 0.9 collective-permute-done.8
  218.7 2.2 collective-permute-start.9
  220.9 5.8 %all-to-all-done.1 = bf16[4,256,1024]{2,1,0:T(8,128)(2,1)S(1)} async-done(((bf16[4,256,1024]{2,1,0:T(8,128)(2,1)}), bf16[4,256,1024]{2,1,0:T(8,128)(2,1)S(1)}, u32[]{:S(2)}, u32[]{:S(2)}) %all-to-all-start.1) | async-done | bytes 2097184 | tf_op jit(solution)/shard_map/all_to_all | solution.py:49
  226.8 0.4 reduce_sum.68
  227.2 1.6 broadcast_in_dim.11
  228.8 3.6 %all-to-all-start.2 = ((bf16[4,256,1024]{2,1,0:T(8,128)(2,1)}), bf16[4,256,1024]{2,1,0:T(8,128)(2,1)S(1)}, u32[]{:S(2)}, u32[]{:S(2)}) async-start(bf16[4,256,1024]{2,1,0:T(8,128)(2,1)} %broadcast_in_dim.11), calls=%async_computation.3 | async-start | bytes 4194304 | tf_op jit(solution)/shard_map/all_to_all | solution.py:53
  232.4 5.5 %fusion.6 = f32[1024,2048]{1,0:T(8,128)} fusion(f32[1024]{0:T(1024)S(1)} %add_rsqrt_fusion, f32[1024]{0:T(1024)S(1)} %broadcast_multiply_fusion, bf16[1032,16,128]{2,0,1:T(8,128)(2,1)} %all-to-all-done), kind=kLoop, calls=%fused_computation.13 | loop fusion | flops 6291456 | bytes 12591104 | tf_op jit(solution)/shard_map/mul | solution.py:91
  238.0 3.6 %collective-permute-start.10 = (f32[2,2048]{1,0:T(2,128)S(1)}, f32[2,2048]{1,0:T(2,128)S(1)}, u32[]{:S(2)}, u32[]{:S(2)}) collective-permute-start(f32[2,2048]{1,0:T(2,128)S(1)} %add.85), channel_id=1, source_target_pairs={{0,64},{32,96},{64,0},{96,32},{1,65},{33,97},{65,1},{97,33},{2,66}... | collective-permute-start | bytes 49160 | tf_op jit(solution)/shard_map/ppermute | solution.py:61
  241.5 14.8 %collective-permute-done.10 = f32[2,2048]{1,0:T(2,128)S(1)} collective-permute-done((f32[2,2048]{1,0:T(2,128)S(1)}, f32[2,2048]{1,0:T(2,128)S(1)}, u32[]{:S(2)}, u32[]{:S(2)}) %collective-permute-start.10) | collective-permute-done | bytes 16416 | tf_op jit(solution)/shard_map/ppermute | solution.py:61
  256.4 0.5 fusion.25
  257.0 0.8 copy.23
  257.9 0.6 bitcast_convert_fusion
  258.5 0.3 mul.187
  258.8 2.1 fusion.32
  260.9 1.7 reshape_reshape.3
  262.5 0.2 mul.190
  262.7 1.4 copy-done
  264.1 2.0 bitcast_multiply_fusion
  266.2 8.6 %reduce-scatter.7.cloned.1.call-done = bf16[128,1024]{1,0:T(8,128)(2,1)} async-done(((bf16[2048,1024]{1,0:T(8,128)(2,1)}), bf16[128,1024]{1,0:T(8,128)(2,1)}) %reduce-scatter.7.cloned.1.call-update) | async-done | bytes 262160
  274.7 1.1 copy.25
  275.9 2.4 add_convert_fusion.4
  (72 shorter events, 1.7 us)
Async XLA Ops:
  11.4 9.1 %copy-start.12 = (s32[8,4]{0,1:T(4,128)S(1)}, s32[8,4]{0,1:T(4,128)}, u32[]{:S(2)}) copy-start(s32[8,4]{0,1:T(4,128)} %param.16) | copy-start | bytes 388
  11.4 9.6 %copy-start.4 = (bf16[1024,512]{1,0:T(8,128)(2,1)S(1)}, bf16[1024,512]{1,0:T(8,128)(2,1)}, u32[]{:S(2)}) copy-start(bf16[1024,512]{1,0:T(8,128)(2,1)} %param.14) | copy-start | bytes 3145732
  11.4 74.8 %all-to-all-start = ((bf16[1032,16,128]{2,0,1:T(8,128)(2,1)}), bf16[1032,16,128]{2,0,1:T(8,128)(2,1)}, u32[]{:S(2)}, u32[]{:S(2)}) async-start(bf16[1032,16,128]{2,0,1:T(8,128)(2,1)} %tile.2), calls=%async_computation | async-start | bytes 8454144 | tf_op jit(solution)/shard_map/all_to_all | solution.py:74
  19.7 93.4 %all-gather.2.cloned.1.call-start = ((), (), s32[]{:S(2)}) async-start(), calls=%async_computation.5 | async-start | bytes 4456448 | tf_op jit(solution)/shard_map/all_gather | solution.py:99
  20.5 173.2 %reduce-scatter.5.cloned.1.call-start = ((), (), s32[]{:S(2)}) async-start(), calls=%async_computation.6 | async-start | bytes 4456448 | tf_op jit(solution)/shard_map/reduce_scatter | solution.py:101
  20.6 0.7 copy-start.13
  21.0 1.2 copy-start.5
  21.2 2.9 %collective-permute-start = (bf16[1024,512]{1,0:T(8,128)(2,1)S(1)}, bf16[1024,512]{1,0:T(8,128)(2,1)}, u32[]{:S(2)}, u32[]{:S(2)}) collective-permute-start(bf16[1024,512]{1,0:T(8,128)(2,1)S(1)} %bitcast_multiply_fusion.3), channel_id=1, source_target_pairs={{0,16},{16,0},{1,17},{17,1},{2,18},{18,2},{3,19},{19,3},{4,20},{20... | collective-permute-start | bytes 3145736 | tf_op jit(solution)/shard_map/ppermute | solution.py:31
  22.4 4.0 %collective-permute-start.1 = (bf16[512,1024]{1,0:T(8,128)(2,1)S(1)}, bf16[512,1024]{1,0:T(8,128)(2,1)}, u32[]{:S(2)}, u32[]{:S(2)}) collective-permute-start(bf16[512,1024]{1,0:T(8,128)(2,1)S(1)} %bitcast_multiply_fusion.2), channel_id=1, source_target_pairs={{0,16},{16,0},{1,17},{17,1},{2,18},{18,2},{3,19},{19,3},{4,20},{20... | collective-permute-start | bytes 3145736 | tf_op jit(solution)/shard_map/ppermute | solution.py:31
  89.2 4.1 %copy-start.6 = (bf16[1024,512]{1,0:T(8,128)(2,1)S(1)}, bf16[1024,512]{1,0:T(8,128)(2,1)}, u32[]{:S(2)}) copy-start(bf16[1024,512]{1,0:T(8,128)(2,1)} %get-tuple-element.45) | copy-start | bytes 3145732
  93.3 11.0 %copy-start.7 = (bf16[512,1024]{1,0:T(8,128)(2,1)S(1)}, bf16[512,1024]{1,0:T(8,128)(2,1)}, u32[]{:S(2)}) copy-start(bf16[512,1024]{1,0:T(8,128)(2,1)} %get-tuple-element.42) | copy-start | bytes 3145732
  93.3 11.0 %copy-start.8 = (bf16[512,1024]{1,0:T(8,128)(2,1)S(1)}, bf16[512,1024]{1,0:T(8,128)(2,1)}, u32[]{:S(2)}) copy-start(bf16[512,1024]{1,0:T(8,128)(2,1)} %get-tuple-element.43) | copy-start | bytes 3145732
  103.3 1.0 copy-start.15
  108.7 0.7 copy-start.11
  108.7 166.0 %reduce-scatter.7.cloned.1.call-start = ((), (), s32[]{:S(2)}) async-start(), calls=%async_computation.7 | async-start | bytes 4456448
  119.8 7.4 %copy-start.17 = (bf16[1024,512]{1,0:T(8,128)(2,1)}, bf16[1024,512]{1,0:T(8,128)(2,1)S(1)}, u32[]{:S(2)}) copy-start(bf16[1024,512]{1,0:T(8,128)(2,1)S(1)} %add_convert_fusion.1) | copy-start | bytes 3145732
  133.6 1.2 copy-start.16
  139.5 1.2 copy-start.18
  139.6 9.8 %collective-permute-start.3 = (bf16[512,1024]{1,0:T(8,128)(2,1)S(1)}, bf16[512,1024]{1,0:T(8,128)(2,1)}, u32[]{:S(2)}, u32[]{:S(2)}) collective-permute-start(bf16[512,1024]{1,0:T(8,128)(2,1)S(1)} %constant_dynamic-slice_fusion.2), channel_id=1, source_target_pairs={{0,16},{16,0},{1,17},{17,1},{2,18},{18,2},{3,19},{19,3},{4,20},{20... | collective-permute-start | bytes 3145736 | tf_op jit(solution)/shard_map/ppermute | solution.py:43
  145.7 1.3 copy-start.1
  148.1 3.0 %collective-permute-start.2 = (bf16[1024,512]{1,0:T(8,128)(2,1)}, bf16[1024,512]{1,0:T(8,128)(2,1)}, u32[]{:S(2)}, u32[]{:S(2)}) collective-permute-start(bf16[1024,512]{1,0:T(8,128)(2,1)} %constant_dynamic-slice_fusion.3), channel_id=1, source_target_pairs={{0,16},{16,0},{1,17},{17,1},{2,18},{18,2},{3,19},{19,3},{4,20},{20... | collective-permute-start | bytes 3145736 | tf_op jit(solution)/shard_map/ppermute | solution.py:43
  148.1 3.0 %copy-start.2 = (bf16[2048,512]{1,0:T(8,128)(2,1)S(1)}, bf16[2048,512]{1,0:T(8,128)(2,1)}, u32[]{:S(2)}) copy-start(bf16[2048,512]{1,0:T(8,128)(2,1)} %copy-done.1) | copy-start | bytes 6291460
  148.1 53.7 %collective-permute-start.4 = (f32[2,3072]{1,0:T(2,128)S(1)}, f32[2,3072]{1,0:T(2,128)S(1)}, u32[]{:S(2)}, u32[]{:S(2)}) collective-permute-start(f32[2,3072]{1,0:T(2,128)S(1)} %maximum_maximum_fusion), channel_id=1, source_target_pairs={{0,1},{1,0},{2,3},{3,2},{4,5},{5,4},{6,7},{7,6},{8,9},{9,8},{10,11... | collective-permute-start | bytes 73736 | tf_op jit(solution)/shard_map/ppermute | solution.py:61
  197.5 20.0 %copy-start.14 = (bf16[128]{0:T(256)(128)(2,1)S(1)}, bf16[128]{0:T(256)(128)(2,1)}, u32[]{:S(2)}) copy-start(bf16[128]{0:T(256)(128)(2,1)} %param.12) | copy-start | bytes 772
  197.5 20.1 %copy-start.9 = (bf16[1024,128]{1,0:T(8,128)(2,1)S(1)}, bf16[1024,128]{1,0:T(8,128)(2,1)}, u32[]{:S(2)}) copy-start(bf16[1024,128]{1,0:T(8,128)(2,1)} %param.9) | copy-start | bytes 786436
  197.5 29.3 %all-to-all-start.1 = ((bf16[4,256,1024]{2,1,0:T(8,128)(2,1)}), bf16[4,256,1024]{2,1,0:T(8,128)(2,1)S(1)}, u32[]{:S(2)}, u32[]{:S(2)}) async-start(bf16[4,256,1024]{2,1,0:T(8,128)(2,1)} %pad_maximum_fusion.2), calls=%async_computation.2 | async-start | bytes 4194304 | tf_op jit(solution)/shard_map/all_to_all | solution.py:49
  201.9 5.6 %collective-permute-start.5 = (f32[2,3072]{1,0:T(2,128)S(1)}, f32[2,3072]{1,0:T(2,128)S(1)}, u32[]{:S(2)}, u32[]{:S(2)}) collective-permute-start(f32[2,3072]{1,0:T(2,128)S(1)} %fusion.40), channel_id=1, source_target_pairs={{0,2},{1,3},{2,0},{3,1},{4,6},{5,7},{6,4},{7,5},{8,10},{9,11},{10,... | collective-permute-start | bytes 73736 | tf_op jit(solution)/shard_map/ppermute | solution.py:61
  207.6 4.1 %collective-permute-start.6 = (f32[2,3072]{1,0:T(2,128)S(1)}, f32[2,3072]{1,0:T(2,128)S(1)}, u32[]{:S(2)}, u32[]{:S(2)}) collective-permute-start(f32[2,3072]{1,0:T(2,128)S(1)} %fusion.41), channel_id=1, source_target_pairs={{0,4},{1,5},{2,6},{3,7},{4,0},{5,1},{6,2},{7,3},{8,12},{9,13},{10,... | collective-permute-start | bytes 73736 | tf_op jit(solution)/shard_map/ppermute | solution.py:61
  211.7 5.7 %collective-permute-start.7 = (f32[2,3072]{1,0:T(2,128)S(1)}, f32[2,3072]{1,0:T(2,128)S(1)}, u32[]{:S(2)}, u32[]{:S(2)}) collective-permute-start(f32[2,3072]{1,0:T(2,128)S(1)} %add.80), channel_id=1, source_target_pairs={{0,8},{1,9},{2,10},{3,11},{4,12},{5,13},{6,14},{7,15},{8,0},{9,1},... | collective-permute-start | bytes 73736 | tf_op jit(solution)/shard_map/ppermute | solution.py:61
  217.4 1.3 collective-permute-start.8
  218.7 19.2 %collective-permute-start.9 = (f32[2,2048]{1,0:T(2,128)S(1)}, f32[2,2048]{1,0:T(2,128)S(1)}, u32[]{:S(2)}, u32[]{:S(2)}) collective-permute-start(f32[2,2048]{1,0:T(2,128)S(1)} %slice_add_fusion), channel_id=1, source_target_pairs={{0,32},{32,0},{64,96},{96,64},{1,33},{33,1},{65,97},{97,65},{2,34}... | collective-permute-start | bytes 49160 | tf_op jit(solution)/shard_map/ppermute | solution.py:61
  228.8 29.1 %all-to-all-start.2 = ((bf16[4,256,1024]{2,1,0:T(8,128)(2,1)}), bf16[4,256,1024]{2,1,0:T(8,128)(2,1)S(1)}, u32[]{:S(2)}, u32[]{:S(2)}) async-start(bf16[4,256,1024]{2,1,0:T(8,128)(2,1)} %broadcast_in_dim.11), calls=%async_computation.3 | async-start | bytes 4194304 | tf_op jit(solution)/shard_map/all_to_all | solution.py:53
  232.4 24.6 %copy-start.3 = (f32[1024,128]{0,1:T(8,128)S(1)}, f32[1024,128]{0,1:T(8,128)}, u32[]{:S(2)}) copy-start(f32[1024,128]{0,1:T(8,128)} %convert_bitcast_fusion.1) | copy-start | bytes 1572868
  238.0 18.4 %collective-permute-start.10 = (f32[2,2048]{1,0:T(2,128)S(1)}, f32[2,2048]{1,0:T(2,128)S(1)}, u32[]{:S(2)}, u32[]{:S(2)}) collective-permute-start(f32[2,2048]{1,0:T(2,128)S(1)} %add.85), channel_id=1, source_target_pairs={{0,64},{32,96},{64,0},{96,32},{1,65},{33,97},{65,1},{97,33},{2,66}... | collective-permute-start | bytes 49160 | tf_op jit(solution)/shard_map/ppermute | solution.py:61
  262.5 1.6 copy-start
  264.1 11.8 %copy-start.10 = (bf16[1024,128]{1,0:T(8,128)(2,1)S(1)}, bf16[1024,128]{1,0:T(8,128)(2,1)}, u32[]{:S(2)}) copy-start(bf16[1024,128]{1,0:T(8,128)(2,1)} %param.10) | copy-start | bytes 786436
Sparse Core Ops, SparseCore 0:
  22.7 90.3 all-gather.1
  116.4 77.2 reduce-scatter.4
  197.4 77.2 reduce-scatter.6
